TPU v7x, 128 devices: a whole 4x4x4 slice. The times are simulated.
128 devices in a mesh: band: 4 (over z), sector: 32 (over y, x, core).
Axes of the slice: x: 4, y: 4, z: 4, core: 2. Of those that a mesh axis runs over, the one named last changes fastest.
Arguments:
- control: float32 [762, 64, 4096], P(None, 'band', 'sector'), may hold values from -16 to 16
- direction: float32 [762, 64, 4096], P(None, 'band', 'sector'), may hold values from -16 to 16
- step_lengths: float32 [4], replicated, may hold values from 0.25 to 2
- level_root: bfloat16 [762, 762], replicated, may hold values from -0.21875 to 0.21875
- lon_decay: float32 [762], replicated, as said below
- lat_decay: float32 [762], replicated, as said below
- obs_operator: bfloat16 [128, 762], replicated, may hold values from -0.21875 to 0.21875
- obs_values: float32 [131072, 128], P(('band', 'sector')), may hold values from -6 to 6
- obs_inv_err: float32 [131072, 128], P(('band', 'sector')), may hold values from 0.5 to 2
- obs_cols: int32 [131072], P(('band', 'sector')), may hold values from 0 to 1918, as said below
- obs_weights: float32 [131072, 4], P(('band', 'sector')), may hold values from 0.1 to 1
- counts: int32 [128, 128], P(('band', 'sector')), may hold values from 1 to 8, as said below
Outputs:
- departures: float32 [131072, 4, 128], P(('band', 'sector'))
- costs: float32 [4], replicated
Inputs may be any that keep to these rules, and one draw needn't show every extreme that they name: `lon_decay`: every line's coefficient lies strictly between 0 and 1. `lat_decay`: every line's coefficient lies strictly between 0 and 1. `obs_cols`: a column lat * 128 + lon of the owner's block with lat <= 14 and lon <= 126; unused slots hold such columns too. `counts`: in every draw some owner receives 8 rows from every device, and some device fills all its slots to every owner.
All inputs are finite; a program needn't handle non-finite values.
Results may differ from a plain program's by a relative error of at most 0.0039.
Values sent between devices are 32-bit elements; how exact they have to be, the bound alone decides.
No kernel may reach another device: no remote copies, remote signals or barrier semaphores. Data moves between devices by JAX's collectives and lax.ppermute only.
A program may use at most 256 MiB of HBM per device.

v0:
```python
import jax
import jax.numpy as jnp
from jax import lax
from jax.sharding import PartitionSpec as P

highest = lax.Precision.HIGHEST


def entering_2(value, axis, join, neutral):
    count, mine = (lax.axis_size(axis), lax.axis_index(axis))
    pieces = jax.tree.map(lambda part: lax.all_gather(part, axis), value)
    so_far = jax.tree.map(
        lambda part, zero: jnp.full_like(part, 0) + jnp.asarray(zero, part.dtype), value, neutral
    )

    def turn(position, so_far):
        longer = join(so_far, jax.tree.map(lambda part: part[position], pieces))
        return jax.tree.map(lambda new, old: jnp.where(position < mine, new, old), longer, so_far)

    return lax.fori_loop(0, count - 1, turn, so_far)


def from_root(block, axis, owner):
    block = jnp.where(lax.axis_index(axis) == owner, block, jnp.zeros_like(block))
    return lax.psum(block, axis)


def compose(earlier, latter):
    return (earlier[0] * latter[0], latter[0] * earlier[1] + latter[1])


def triangle(log_rate, length):
    position = jnp.arange(length)
    offset = (position[:, None] - position[None, :]).astype(jnp.float32)
    powers = jnp.exp(log_rate[:, None, None] * jnp.maximum(offset, 0.0)[None])
    return jnp.where(offset[None] >= 0.0, powers, 0.0)


def rising(log_rate, length):
    return jnp.exp(log_rate[:, None] * jnp.arange(1, length + 1).astype(jnp.float32)[None, :])


def body(
    control,
    direction,
    step_lengths,
    level_root,
    lon_decay,
    lat_decay,
    obs_operator,
    obs_values,
    obs_inv_err,
    obs_cols,
    obs_weights,
    counts,
):
    num_lines, lat_dev, lon_dev = control.shape
    trials_count = step_lengths.shape[0]
    channels = obs_values.shape[1]
    bands = lax.axis_size("band")
    sectors = lax.axis_size("sector")
    devices_all = bands * sectors
    capacity = obs_cols.shape[0] // devices_all
    trial_fields = control[None] + step_lengths[:, None, None, None] * direction[None]
    background = jnp.sum(trial_fields * trial_fields, axis=(1, 2, 3))
    mixed_field = jnp.einsum(
        "kl,tlab->tkab",
        level_root,
        trial_fields.astype(jnp.bfloat16),
        preferred_element_type=jnp.float32,
    )
    log_lon = jnp.log(lon_decay)
    local_lon = jnp.einsum(
        "lij,tlaj->tlai", triangle(log_lon, lon_dev), mixed_field, precision=highest
    )
    lon_states = local_lon[:, :, :, -1].reshape(trials_count, num_lines * lat_dev)
    lon_step = jnp.repeat(log_lon * lon_dev, lat_dev)
    loop_gain = 1.0 - jnp.exp(lon_step * sectors)
    step_map = jnp.exp(lon_step)
    prefix_map, prefix_sum = entering_2(
        (step_map, lon_states),
        "sector",
        compose,
        (jnp.ones_like(step_map), jnp.zeros_like(lon_states)),
    )
    whole_sum = compose((prefix_map, prefix_sum), (step_map, lon_states))[1]
    loop_sum = from_root(whole_sum, "sector", sectors - 1)
    incoming = prefix_sum + prefix_map * loop_sum / loop_gain
    incoming = incoming.reshape(trials_count, num_lines, lat_dev)
    lon_field = local_lon + rising(log_lon, lon_dev)[None, :, None, :] * incoming[:, :, :, None]
    lon_field = lon_field * jnp.sqrt(1.0 - lon_decay * lon_decay)[None, :, None, None]
    log_lat = jnp.log(lat_decay)
    local_lat = jnp.einsum(
        "lij,tljb->tlib", triangle(log_lat, lat_dev), lon_field, precision=highest
    )
    lat_states = local_lat[:, :, -1, :].reshape(trials_count, num_lines * lon_dev)
    lat_step = jnp.exp(jnp.repeat(log_lat * lat_dev, lon_dev))
    unused, entering = entering_2(
        (lat_step, lat_states),
        "band",
        compose,
        (jnp.ones_like(lat_step), jnp.zeros_like(lat_states)),
    )
    entering = entering.reshape(trials_count, num_lines, lon_dev)
    increment = local_lat + rising(log_lat, lat_dev)[None, :, :, None] * entering[:, :, None, :]
    increment = increment * jnp.sqrt(1.0 - lat_decay * lat_decay)[None, :, None, None]
    columns = increment.reshape(trials_count, num_lines, lat_dev * lon_dev)
    targets = obs_cols.reshape(devices_all, capacity)
    weights = obs_weights.reshape(devices_all, capacity, 4)
    observed = obs_values.reshape(devices_all, capacity, channels)
    evolve_targets = lax.all_to_all(
        targets, ("band", "sector"), split_axis=0, concat_axis=0, tiled=True
    )
    evolve_weights = lax.all_to_all(
        weights, ("band", "sector"), split_axis=0, concat_axis=0, tiled=True
    )
    flat_targets = evolve_targets.reshape(-1)
    flat_weights = evolve_weights.reshape(-1, 4)
    profile = jnp.zeros((trials_count, num_lines, flat_targets.shape[0]), jnp.float32)
    for corner, offset in enumerate((0, 1, lon_dev, lon_dev + 1)):
        profile = profile + flat_weights[:, corner] * jnp.take(
            columns, flat_targets + offset, axis=2
        )
    evolved = jnp.einsum(
        "tlr,cl->rtc",
        profile.astype(jnp.bfloat16),
        obs_operator,
        preferred_element_type=jnp.float32,
    )
    misfit_rows = (
        evolved.reshape(evolve_targets.shape + (trials_count, channels))
        - lax.all_to_all(observed, ("band", "sector"), split_axis=0, concat_axis=0, tiled=True)[
            :, :, None, :
        ]
    )
    returned = lax.all_to_all(
        misfit_rows, ("band", "sector"), split_axis=0, concat_axis=0, tiled=True
    )
    live_slot = counts[0][:, None] > jnp.arange(capacity, dtype=jnp.int32)[None, :]
    weighted = returned * obs_inv_err.reshape(devices_all, capacity, 1, channels)
    departures = jnp.where(live_slot[:, :, None, None], weighted, 0.0)
    misfit = jnp.sum(departures * departures, axis=(0, 1, 3))
    totals = lax.psum((background, misfit), ("band", "sector"))
    cell_count = num_lines * lat_dev * lon_dev * devices_all
    cost_values = 0.5 * (totals[0] + totals[1]) / cell_count
    return (departures.reshape(devices_all * capacity, trials_count, channels), cost_values)


def solution(mesh):
    placed = (
        P(None, "band", "sector"),
        P(None, "band", "sector"),
        P(),
        P(),
        P(),
        P(),
        P(),
        P(("band", "sector"), None),
        P(("band", "sector"), None),
        P(("band", "sector")),
        P(("band", "sector"), None),
        P(("band", "sector"), None),
    )
    return jax.shard_map(
        body,
        mesh=mesh,
        in_specs=placed,
        out_specs=(P(("band", "sector"), None, None), P()),
        check_vma=False,
    )
```

profile of v0, /device:TPU:0, one launch (start us, length us, event | category | flops | bytes accessed | tf_op | source)
XLA Modules:
  0.0 808.5 jit_solution(14113501835075006201)
XLA Ops:
  9.9 6.6 copy.64
  16.6 6.8 copy.65
  23.3 17.4 %fusion.34 = f32[4,762,16,128]{1,3,2,0:T(8,128)} fusion(f32[762,16,128]{0,2,1:T(8,128)} %copy.65, f32[4]{0:T(128)S(1)} %copy-done.5, f32[762,16,128]{0,2,1:T(8,128)} %copy.64, bf16[762,762]{1,0:T(8,128)(2,1)S(1)} %copy-done), kind=kOutput, calls=%fused_computation.45 | convolution fusion | flops 9531998208 | bytes 38615128 | tf_op jit(solution)/shard_map/kl,tlab->tkab/dot_general | solution.py:66
  40.7 24.9 %copy.66 = f32[4,762,16,128]{3,2,0,1:T(8,128)} copy(f32[4,762,16,128]{1,3,2,0:T(8,128)} %fusion.34) | data formatting | bytes 49938432 | tf_op jit(solution)/shard_map/kl,tlab->tkab/transpose | solution.py:66
  65.7 97.7 %fusion.31 = f32[4,762,16,128]{3,2,0,1:T(8,128)S(1)} fusion(f32[4,762,16,128]{3,2,0,1:T(8,128)} %copy.66, f32[128,128]{1,0:T(8,128)S(1)} %convert_maximum_fusion, f32[762]{0:T(1024)S(1)} %get-tuple-element.296, pred[128,128]{1,0:T(8,128)(4,1)S(1)} %convert_compare_fusion), kind=kOutput, calls=%fused_computation.44 | convolution fusion | flops 9613148160 | bytes 50023400 | tf_op jit(solution)/shard_map/lij,tlaj->tlai/dot_general | solution.py:73
  163.4 8.2 %copy-done.2 = f32[4,762,16,128]{3,2,0,1:T(8,128)} copy-done((f32[4,762,16,128]{3,2,0,1:T(8,128)}, f32[4,762,16,128]{3,2,0,1:T(8,128)S(1)}, u32[]{:S(2)}) %copy-start.2) | copy-done | bytes 24969240
  171.6 10.6 %slice.33 = f32[4,762,16,1]{3,2,0,1:T(8,128)} slice(f32[4,762,16,128]{3,2,0,1:T(8,128)S(1)} %fusion.31), slice={[0:4], [0:762], [0:16], [127:128]} | slice | bytes 390144 | tf_op jit(solution)/shard_map/slice | solution.py:76
  182.2 21.2 %copy.67 = f32[4,762,16,1]{2,1,0,3:T(8,128)S(1)} copy(f32[4,762,16,1]{3,2,0,1:T(8,128)} %slice.33) | data formatting | bytes 390144 | tf_op jit(solution)/shard_map/slice | solution.py:76
  203.4 1.5 all_gather_reshape_squeeze.6
  206.0 2.3 copy.100
  208.3 48.1 %all-gather.7.cloned.1.call-done = f32[32,4,12192]{2,1,0:T(4,128)} async-done(((f32[1,4,12192]{2,1,0:T(4,128)}), f32[32,4,12192]{2,1,0:T(4,128)}) %all-gather.7.cloned.1.call-update) | async-done | bytes 6242320 | tf_op jit(solution)/shard_map/all_gather | solution.py:11
  256.4 39.2 %while.30 = (s32[]{:T(128)}, f32[12192]{0:T(1024)S(1)}, f32[4,12192]{1,0:T(4,128)S(1)}, s32[]{:T(128)}, f32[32,12192]{1,0:T(8,128)S(1)}, /*index=5*/f32[32,4,12192]{2,1,0:T(4,128)}, s32[]{:T(128)}, s32[]{:T(128)}) while((s32[]{:T(128)}, f32[12192]{0:T(1024)S(1)}, f32[4,12192]{1,0:T(4,128)S(1)}, s32[]{:T(128)}, ...), condition=%wide.region_1.2_spmd.clone, body=%wide.region_0.0_spmd.clone.sunk | while | flops 231652 | bytes 877947 | solution.py:20
  256.5 1.2 fusion.67
  257.8 1.2 fusion.67
  259.0 1.2 fusion.67
  260.3 1.2 fusion.67
  298.4 98.0 %all-reduce.2.cloned.1.call-done = f32[4,12192]{1,0:T(4,128)} async-done(((f32[4,12192]{1,0:T(4,128)}), f32[4,12192]{1,0:T(4,128)}) %all-reduce.2.cloned.1.call-update) | async-done | bytes 195088 | tf_op jit(solution)/shard_map/psum | solution.py:25
  398.9 30.7 %fusion.28 = f32[4,762,16,128]{3,2,0,1:T(8,128)} fusion(f32[4,762,16,128]{3,2,0,1:T(8,128)} %copy-done.2, f32[762]{0:T(1024)S(1)} %get-tuple-element.297, f32[4,762,16]{2,0,1:T(4,128)S(1)} %copy.69, f32[762,128]{1,0:T(8,128)S(1)} %multiply_exponential_fusion, f32[16,16]{1,0:T(8,128)S(1)} %convert_maximum_fusion.1, f32[762]{0:T(1024)S(1)} %get-tuple-element.291, ...), kind=kOutput, calls=%fused_computation.43 | convolution fusion | flops 1217639424 | bytes 50531024 | tf_op jit(solution)/shard_map/lij,tljb->tlib/dot_general | solution.py:93
  429.6 7.4 slice.34
  437.7 7.8 all-to-all-start.1
  446.9 8.0 all-to-all-done.1
  454.8 4.8 all-to-all-start
  461.1 9.3 %all-to-all-done = f32[128,8,4]{1,2,0:T(4,128)S(1)} async-done(((f32[128,8,4]{1,2,0:T(4,128)}), f32[128,8,4]{1,2,0:T(4,128)S(1)}, u32[]{:S(2)}, u32[]{:S(2)}) %all-to-all-start) | async-done | bytes 16416 | tf_op jit(solution)/shard_map/all_to_all | solution.py:114
  470.3 5.9 all-to-all-start.2
  476.5 3.0 copy.101
  479.5 31.0 %all-gather.9.cloned.1.call-done = f32[4,4,97536]{2,1,0:T(4,128)} async-done(((f32[1,4,97536]{2,1,0:T(4,128)}), f32[4,4,97536]{2,1,0:T(4,128)}) %all-gather.9.cloned.1.call-update) | async-done | bytes 6242320 | tf_op jit(solution)/shard_map/all_gather | solution.py:11
  510.5 14.6 %while.31 = (s32[]{:T(128)}, f32[4,97536]{1,0:T(4,128)S(1)}, s32[]{:T(128)}, f32[4,97536]{1,0:T(4,128)}, f32[4,4,97536]{2,1,0:T(4,128)}, /*index=5*/s32[]{:T(128)}, s32[]{:T(128)}) while((s32[]{:T(128)}, f32[4,97536]{1,0:T(4,128)S(1)}, s32[]{:T(128)}, f32[4,97536]{1,0:T(4,128)}, f32[4,4,97536]{2,1,0:T(4,128)}, ...), condition=%wide.region_4.5_spmd.clone, body=%wide.region_3.4_spmd.clone.sunk | while | flops 1560580 | bytes 5852273 | solution.py:20
  510.5 2.5 dynamic-slice_reduce_fusion.2
  513.0 2.3 fusion.68
  515.4 2.5 dynamic-slice_reduce_fusion.2
  517.9 2.3 fusion.68
  520.3 2.5 dynamic-slice_reduce_fusion.2
  522.8 2.3 fusion.68
  525.1 19.2 %add_multiply_fusion = f32[4,762,16,128]{3,2,0,1:T(8,128)} fusion(f32[4,762,16,128]{3,2,0,1:T(8,128)} %fusion.28, f32[762]{0:T(1024)S(1)} %get-tuple-element.290, f32[4,762,128]{2,0,1:T(4,128)S(1)} %bitcast.103, f32[762,16]{1,0:T(8,128)S(1)} %copy.70), kind=kLoop, calls=%fused_computation.19 | loop fusion | flops 18726912 | bytes 51550824 | tf_op jit(solution)/shard_map/mul | solution.py:106
  544.3 25.7 %copy.83 = f32[4,762,16,128]{1,0,3,2:T(4,128)} copy(f32[4,762,16,128]{3,2,0,1:T(8,128)} %add_multiply_fusion) | data formatting | bytes 49938432 | tf_op jit(solution)/shard_map/reshape | solution.py:107
  570.0 25.1 %gather_fusion.3 = f32[1024,4,762]{2,1,0:T(4,128)} fusion(f32[4,762,2048]{1,0,2:T(4,128)} %bitcast.99, s32[1024]{0:T(1024)S(1)} %get-tuple-element.288), kind=kCustom, calls=%fused_computation.3.clone | custom fusion | bytes 24973312 | tf_op jit(solution)/shard_map/jit(_take)/gather | solution.py:121
  595.0 25.0 %gather_fusion.2 = f32[1024,4,762]{2,1,0:T(4,128)} fusion(f32[4,762,2048]{1,0,2:T(4,128)} %bitcast.100, s32[1024]{0:T(1024)S(1)} %get-tuple-element.287), kind=kCustom, calls=%fused_computation.2.clone | custom fusion | bytes 24973312 | tf_op jit(solution)/shard_map/jit(_take)/gather | solution.py:121
  620.0 24.9 %gather_fusion.1 = f32[1024,4,762]{2,1,0:T(4,128)} fusion(f32[4,762,2048]{1,0,2:T(4,128)} %bitcast.101, s32[1024]{0:T(1024)S(1)} %get-tuple-element.286), kind=kCustom, calls=%fused_computation.1.clone | custom fusion | bytes 24973312 | tf_op jit(solution)/shard_map/jit(_take)/gather | solution.py:121
  644.9 25.0 %gather_fusion = f32[1024,4,762]{2,1,0:T(4,128)} fusion(f32[4,762,2048]{1,0,2:T(4,128)} %bitcast.102, s32[1024]{0:T(1024)S(1)} %get-tuple-element.285), kind=kCustom, calls=%fused_computation.clone | custom fusion | bytes 24973312 | tf_op jit(solution)/shard_map/jit(_take)/gather | solution.py:121
  669.9 17.8 %fusion.19 = bf16[4,762,1024]{1,0,2:T(4,128)(2,1)S(1)} fusion(f32[1024,4,762]{2,1,0:T(4,128)} %gather_fusion.3, f32[1024,4,762]{2,1,0:T(4,128)} %gather_fusion.2, f32[1024,4,762]{2,1,0:T(4,128)} %gather_fusion.1, f32[1024,4,762]{2,1,0:T(4,128)} %gather_fusion, f32[1024]{0:T(1024)S(1)} %bitcast.111, f32[1024]{0:T(1024)S(1)} %bitcast.112, ...), kind=kLoop, calls=%fused_computation.31 | loop fusion | flops 37453824 | bytes 56201216 | tf_op jit(solution)/shard_map/convert_element_type | solution.py:126
  687.8 1.8 fusion.49
  689.6 2.8 copy_subtract_fusion
  692.4 8.6 %all-to-all-start.3 = ((f32[128,8,4,128]{3,1,2,0:T(8,128)}), f32[128,8,4,128]{3,1,2,0:T(8,128)S(1)}, u32[]{:S(2)}, u32[]{:S(2)}) async-start(f32[128,8,4,128]{3,1,2,0:T(8,128)} %copy_subtract_fusion), calls=%async_computation.3 | async-start | bytes 4194304 | tf_op jit(solution)/shard_map/all_to_all | solution.py:136
  701.1 9.4 %multiply_reduce_fusion = f32[4]{0:T(128)S(1)} fusion(f32[762,16,128]{0,2,1:T(8,128)} %copy.65, f32[4]{0:T(128)S(1)} %copy-done.6, f32[762,16,128]{0,2,1:T(8,128)} %copy.64), kind=kLoop, calls=%fused_computation.16 | loop fusion | flops 24969212 | bytes 12484640 | tf_op jit(solution)/shard_map/reduce_sum | solution.py:65
  710.5 20.8 %all-to-all-done.3 = f32[128,8,4,128]{3,1,2,0:T(8,128)S(1)} async-done(((f32[128,8,4,128]{3,1,2,0:T(8,128)}), f32[128,8,4,128]{3,1,2,0:T(8,128)S(1)}, u32[]{:S(2)}, u32[]{:S(2)}) %all-to-all-start.3) | async-done | bytes 2097184 | tf_op jit(solution)/shard_map/all_to_all | solution.py:136
  731.3 2.7 multiply_reduce_fusion.1
  734.1 62.3 %psum.24 = f32[4]{0:T(128)S(1)} all-reduce(f32[4]{0:T(128)S(1)} %add.155), channel_id=1, replica_groups=mesh['band'=4,'sector'=32] {'band','sector'}, use_global_device_ids=true, to_apply=%region_6.8 | all-reduce | flops 4 | bytes 32 | tf_op jit(solution)/shard_map/psum | solution.py:143
  796.9 4.3 copy.79
  (158 shorter events, 46.1 us)
Async XLA Ops:
  8.0 15.3 %copy-start = (bf16[762,762]{1,0:T(8,128)(2,1)S(1)}, bf16[762,762]{1,0:T(8,128)(2,1)}, u32[]{:S(2)}) copy-start(bf16[762,762]{1,0:T(8,128)(2,1)} %param.21) | copy-start | bytes 3483868
  8.0 198.0 %all-gather.11.cloned.1.call-start = ((), (), s32[]{:S(2)}) async-start(), calls=%async_computation.7 | async-start | bytes 1622016 | tf_op jit(solution)/shard_map/all_gather | solution.py:11
  9.8 13.5 %copy-start.5 = (f32[4]{0:T(128)S(1)}, f32[4]{0:T(128)}, u32[]{:S(2)}) copy-start(f32[4]{0:T(128)} %param.20) | copy-start | bytes 52
  9.9 246.6 %all-gather.7.cloned.1.call-start = ((), (), s32[]{:S(2)}) async-start(), calls=%async_computation.4 | async-start | bytes 6488064 | tf_op jit(solution)/shard_map/all_gather | solution.py:11
  163.4 8.2 %copy-start.2 = (f32[4,762,16,128]{3,2,0,1:T(8,128)}, f32[4,762,16,128]{3,2,0,1:T(8,128)S(1)}, u32[]{:S(2)}) copy-start(f32[4,762,16,128]{3,2,0,1:T(8,128)S(1)} %fusion.31) | copy-start | bytes 74907648
  204.9 191.4 %all-reduce.2.cloned.1.call-start = ((), (), s32[]{:S(2)}) async-start(), calls=%async_computation.5 | async-start | bytes 393216 | tf_op jit(solution)/shard_map/psum | solution.py:25
  296.4 180.1 %all-gather.13.cloned.1.call-start = ((), (), s32[]{:S(2)}) async-start(), calls=%async_computation.8 | async-start | bytes 1950720 | tf_op jit(solution)/shard_map/all_gather | solution.py:11
  297.8 212.7 %all-gather.9.cloned.1.call-start = ((), (), s32[]{:S(2)}) async-start(), calls=%async_computation.6 | async-start | bytes 7802880 | tf_op jit(solution)/shard_map/all_gather | solution.py:11
  398.9 38.1 %copy-start.7 = (s32[1024]{0:T(1024)S(1)}, s32[1024]{0:T(1024)}, u32[]{:S(2)}) copy-start(s32[1024]{0:T(1024)} %param.27) | copy-start | bytes 12292
  398.9 46.7 %copy-start.4 = (f32[1024,4]{0,1:T(4,128)S(1)}, f32[1024,4]{0,1:T(4,128)}, u32[]{:S(2)}) copy-start(f32[1024,4]{0,1:T(4,128)} %param.28) | copy-start | bytes 49156
  437.7 17.1 %all-to-all-start.1 = ((s32[128,1,8]{2,1,0:T(1,128)}), s32[128,1,8]{2,1,0:T(1,128)S(1)}, u32[]{:S(2)}, u32[]{:S(2)}) async-start(s32[128,1,8]{2,1,0:T(1,128)} %bitcast.2), calls=%async_computation.1 | async-start | bytes 131072 | tf_op jit(solution)/shard_map/all_to_all | solution.py:111
  454.8 15.5 %all-to-all-start = ((f32[128,8,4]{1,2,0:T(4,128)}), f32[128,8,4]{1,2,0:T(4,128)S(1)}, u32[]{:S(2)}, u32[]{:S(2)}) async-start(f32[128,8,4]{1,2,0:T(4,128)} %copy.61), calls=%async_computation | async-start | bytes 524288 | tf_op jit(solution)/shard_map/all_to_all | solution.py:114
  470.3 219.2 %all-to-all-start.2 = ((f32[128,8,128]{2,1,0:T(8,128)}), f32[128,8,128]{2,1,0:T(8,128)}, u32[]{:S(2)}, u32[]{:S(2)}) async-start(f32[128,8,128]{2,1,0:T(8,128)} %bitcast.24), calls=%async_computation.2 | async-start | bytes 1048576 | tf_op jit(solution)/shard_map/all_to_all | solution.py:132
  669.9 17.8 %copy-start.3 = (bf16[128,762]{1,0:T(8,128)(2,1)S(1)}, bf16[128,762]{1,0:T(8,128)(2,1)}, u32[]{:S(2)}) copy-start(bf16[128,762]{1,0:T(8,128)(2,1)} %param.24) | copy-start | bytes 585220
  687.8 13.2 %copy-start.8 = (s32[1,128]{1,0:T(1,128)S(1)}, s32[1,128]{1,0:T(1,128)}, u32[]{:S(2)}) copy-start(s32[1,128]{1,0:T(1,128)} %param.29) | copy-start | bytes 1540
  687.8 13.3 %copy-start.6 = (f32[4]{0:T(128)S(1)}, f32[4]{0:T(128)}, u32[]{:S(2)}) copy-start(f32[4]{0:T(128)} %param.20) | copy-start | bytes 52
  689.6 111.5 %copy-start.1 = (bf16[762,762]{1,0:T(8,128)(2,1)S(1)}, bf16[762,762]{1,0:T(8,128)(2,1)}, u32[]{:S(2)}) copy-start(bf16[762,762]{1,0:T(8,128)(2,1)} %param.21) | copy-start | bytes 3483868
  692.4 38.9 %all-to-all-start.3 = ((f32[128,8,4,128]{3,1,2,0:T(8,128)}), f32[128,8,4,128]{3,1,2,0:T(8,128)S(1)}, u32[]{:S(2)}, u32[]{:S(2)}) async-start(f32[128,8,4,128]{3,1,2,0:T(8,128)} %copy_subtract_fusion), calls=%async_computation.3 | async-start | bytes 4194304 | tf_op jit(solution)/shard_map/all_to_all | solution.py:136
Sparse Core Ops, SparseCore 0:
  11.1 45.2 all-gather.10
  205.0 51.3 all-gather.6
  296.5 99.7 all-reduce.1
Sparse Core Ops, SparseCore 1:
  299.1 25.3 all-gather.12
  437.1 73.3 all-gather.8
where the time goes:
time: 815 us; the launch traced here: 808 us
  local copies, waits for them, and re-layouts  239 us (29%)
  waiting for transfers between devices  215 us (26%)
  matrix products  148 us (18%)
  other arithmetic  100 us (12%)
  blocking collectives  62.3 us (8%)
  starting transfers between devices  27.3 us (3%)
  between operations  15.8 us (2%)
    gather x4, local copies, waits for them, and re-layouts, body(): jnp.take(columns, flat_targets + offset, axis=2)  100 us
    psum x1, waiting for transfers between devices, from_root(): return lax.psum(block, axis)  98 us
    dot_general x1, matrix products, body(): jnp.einsum('lij,tlaj->tlai', triangle(log_lon, lon_dev), mixed_field, pre...  97.7 us
    all_gather x4, waiting for transfers between devices, entering_2(): pieces = jax.tree.map(lambda part: lax.all_gather(part, axis), value)  79.2 us
    psum x1, blocking collectives, body(): totals = lax.psum((background, misfit), ('band', 'sector'))  62.3 us
    select_n x65, other arithmetic, turn(): jnp.where(position < mine, new, old)  43.9 us
    unnamed x25, local copies, waits for them, and re-layouts  33.2 us
    slice x2, local copies, waits for them, and re-layouts, body(): local_lon[:, :, :, -1].reshape(trials_count, num_lines * lat_dev)  31.7 us
  transfers between devices with their start and end apart: 9, of which 6 were waited for; matrix products, arithmetic and copies ran while one was open for 53% of the time, Pallas kernels for 0%

commit v1 on v0

v1 whole, which is shorter than its diff:
```python
import functools

import jax
import jax.numpy as jnp
from jax import lax
from jax.experimental import pallas as pl
from jax.experimental.pallas import tpu as pltpu
from jax.sharding import PartitionSpec as P

LANES = 128
SCAN_STEPS = 7
LINE_TILE = 256


def padded_lines(n):
    return -(-n // LINE_TILE) * LINE_TILE


def local_filter_kernel(lat_groups, mix_ref, x_ref, apow_ref, lat_ref, out_ref, end_ref):
    tile = mix_ref.shape[0]
    lane = lax.broadcasted_iota(jnp.int32, (tile, LANES), 1)
    decay = lat_ref[...]
    weights = mix_ref[...]
    state = None
    ends = jnp.zeros((tile, LANES), jnp.float32)
    for g in range(lat_groups):
        cols = pl.ds(g * LANES, LANES)
        v = jnp.dot(weights, x_ref[0, :, cols], preferred_element_type=jnp.float32)
        for s in range(SCAN_STEPS):
            shift = 1 << s
            moved = pltpu.roll(v, shift, 1)
            v = v + jnp.where(lane >= shift, apow_ref[s] * moved, 0.0)
        last = jnp.sum(jnp.where(lane == LANES - 1, v, 0.0), axis=1, keepdims=True)
        ends = jnp.where(lane == g, last, ends)
        state = v if state is None else decay * state + v
        out_ref[0, :, cols] = state
    end_ref[0] = ends


def local_filter(mix, xb, apow, lat_b):
    trials, kpad, cols = xb.shape
    groups = cols // LANES
    tiles = kpad // LINE_TILE
    flops = 2 * kpad * kpad * cols * trials + 30 * trials * kpad * cols
    bytes_accessed = xb.size * 2 + trials * kpad * cols * 4 + mix.size * 2 * trials
    return pl.pallas_call(
        functools.partial(local_filter_kernel, groups),
        grid=(trials, tiles),
        in_specs=[
            pl.BlockSpec((LINE_TILE, kpad), lambda t, k: (k, 0)),
            pl.BlockSpec((1, kpad, cols), lambda t, k: (t, 0, 0)),
            pl.BlockSpec((SCAN_STEPS, LINE_TILE, LANES), lambda t, k: (0, k, 0)),
            pl.BlockSpec((LINE_TILE, LANES), lambda t, k: (k, 0)),
        ],
        out_specs=[
            pl.BlockSpec((1, LINE_TILE, cols), lambda t, k: (t, k, 0)),
            pl.BlockSpec((1, LINE_TILE, LANES), lambda t, k: (t, k, 0)),
        ],
        out_shape=[
            jax.ShapeDtypeStruct((trials, kpad, cols), jnp.float32),
            jax.ShapeDtypeStruct((trials, kpad, LANES), jnp.float32),
        ],
        compiler_params=pltpu.CompilerParams(dimension_semantics=("arbitrary", "arbitrary")),
        cost_estimate=pl.CostEstimate(
            flops=flops, bytes_accessed=bytes_accessed, transcendentals=0
        ),
    )(mix, xb, apow, lat_b)


def shifted(x, axis, shift):
    n = lax.axis_size(axis)
    return lax.ppermute(x, axis, [(s, (s + shift) % n) for s in range(n)])


def xor_total(x, axes):
    for axis in axes:
        n = lax.axis_size(axis)
        bit = 1
        while bit < n:
            x = x + lax.ppermute(x, axis, [(s, s ^ bit) for s in range(n)])
            bit *= 2
    return x


def body(
    control,
    direction,
    step_lengths,
    level_root,
    lon_decay,
    lat_decay,
    obs_operator,
    obs_values,
    obs_inv_err,
    obs_cols,
    obs_weights,
    counts,
):
    num_lines, lat_dev, lon_dev = control.shape
    trials = step_lengths.shape[0]
    channels = obs_values.shape[1]
    bands = lax.axis_size("band")
    sectors = lax.axis_size("sector")
    devices_all = bands * sectors
    capacity = obs_cols.shape[0] // devices_all
    kpad = padded_lines(num_lines)
    extra = kpad - num_lines
    f32 = jnp.float32

    packed = jnp.concatenate(
        [obs_cols.astype(f32)[:, None], obs_weights], axis=1
    ).reshape(devices_all, capacity, 5)
    packed = lax.all_to_all(packed, ("band", "sector"), 0, 0, tiled=True)

    trial_fields = control[None] + step_lengths[:, None, None, None] * direction[None]
    background = jnp.sum(trial_fields * trial_fields, axis=(1, 2, 3))
    xb = trial_fields.astype(jnp.bfloat16).reshape(trials, num_lines, lat_dev * lon_dev)
    xb = jnp.pad(xb, ((0, 0), (0, extra), (0, 0)))
    mix = jnp.pad(level_root, ((0, extra), (0, extra)))

    a = jnp.pad(lon_decay, (0, extra), constant_values=0.5)
    b = jnp.pad(lat_decay, (0, extra), constant_values=0.5)
    log_a = jnp.log(a)
    log_b = jnp.log(b)
    spans = (2.0 ** jnp.arange(SCAN_STEPS)).astype(f32)
    apow = jnp.exp(spans[:, None] * log_a[None, :])
    apow = jnp.broadcast_to(apow[:, :, None], (SCAN_STEPS, kpad, LANES))
    lat_b = jnp.broadcast_to(b[:, None], (kpad, LANES))

    local, ends = local_filter(mix, xb, apow, lat_b)
    local = local.reshape(trials, kpad, lat_dev, lon_dev)
    lon_ends = ends[:, :, :lat_dev]

    sector_gain = jnp.exp(log_a * lon_dev)
    carried = shifted(lon_ends, "sector", 1)
    carried = carried + sector_gain[None, :, None] * shifted(lon_ends, "sector", 2)
    span = 2
    while span < sectors:
        gain = jnp.exp(log_a * (lon_dev * span))
        carried = carried + gain[None, :, None] * shifted(carried, "sector", span)
        span *= 2
    loop_gain = 1.0 - jnp.exp(log_a * (lon_dev * sectors))
    incoming = carried / loop_gain[None, :, None]

    rows = []
    state = jnp.zeros((trials, kpad), f32)
    for i in range(lat_dev):
        state = b[None, :] * state + incoming[:, :, i]
        rows.append(state)
    incoming_lat = jnp.stack(rows, axis=2)
    lon_rise = jnp.exp(log_a[:, None] * jnp.arange(1, lon_dev + 1).astype(f32)[None, :])
    lat_rise = jnp.exp(log_b[:, None] * jnp.arange(1, lat_dev + 1).astype(f32)[None, :])
    scale_a = jnp.sqrt(1.0 - a * a)
    scale_b = jnp.sqrt(1.0 - b * b)

    band_end = scale_a[None, :, None] * (
        local[:, :, lat_dev - 1, :] + lon_rise[None] * incoming_lat[:, :, lat_dev - 1, None]
    )
    band_ends = lax.all_gather(band_end, "band")
    me = lax.axis_index("band")
    source = jnp.arange(bands)
    power = (me - 1 - source).astype(f32)
    band_weight = jnp.where(
        (source < me)[:, None], jnp.exp(log_b[None, :] * (lat_dev * power)[:, None]), 0.0
    )
    entering = jnp.sum(band_weight[:, None, :, None] * band_ends, axis=0)

    increment = scale_b[None, :, None, None] * (
        scale_a[None, :, None, None]
        * (local + lon_rise[None, :, None, :] * incoming_lat[:, :, :, None])
        + lat_rise[None, :, :, None] * entering[:, :, None, :]
    )
    table = jnp.transpose(increment, (2, 3, 0, 1)).reshape(lat_dev * lon_dev, trials * kpad)

    where = packed[:, :, 0].astype(jnp.int32).reshape(-1)
    weights = packed[:, :, 1:].reshape(-1, 4)
    profile = None
    for corner, offset in enumerate((0, 1, lon_dev, lon_dev + 1)):
        picked = table.at[where + offset].get(mode="promise_in_bounds")
        term = weights[:, corner, None] * picked
        profile = term if profile is None else profile + term
    profile = profile.reshape(-1, trials, kpad).astype(jnp.bfloat16)
    operator = jnp.pad(obs_operator, ((0, 0), (0, extra)))
    evolved = jnp.einsum(
        "rtk,ck->rtc", profile, operator, preferred_element_type=f32
    ).reshape(devices_all, capacity, trials, channels)
    returned = lax.all_to_all(evolved, ("band", "sector"), 0, 0, tiled=True)

    observed = obs_values.reshape(devices_all, capacity, 1, channels)
    inverse = obs_inv_err.reshape(devices_all, capacity, 1, channels)
    live = counts[0][:, None] > jnp.arange(capacity, dtype=jnp.int32)[None, :]
    weighted = (returned - observed) * inverse
    departures = jnp.where(live[:, :, None, None], weighted, 0.0)
    misfit = jnp.sum(departures * departures, axis=(0, 1, 3))

    totals = xor_total(jnp.stack([background, misfit]), ("sector", "band"))
    cell_count = num_lines * lat_dev * lon_dev * devices_all
    cost_values = 0.5 * (totals[0] + totals[1]) / cell_count
    return (departures.reshape(devices_all * capacity, trials, channels), cost_values)


def solution(mesh):
    placed = (
        P(None, "band", "sector"),
        P(None, "band", "sector"),
        P(),
        P(),
        P(),
        P(),
        P(),
        P(("band", "sector"), None),
        P(("band", "sector"), None),
        P(("band", "sector")),
        P(("band", "sector"), None),
        P(("band", "sector"), None),
    )
    return jax.shard_map(
        body,
        mesh=mesh,
        in_specs=placed,
        out_specs=(P(("band", "sector"), None, None), P()),
        check_vma=False,
    )
```

time: 815 us -> 574 us (0.70)
  Pallas kernels: 0 us -> 120 us
  matrix products: 148 us -> 57.7 us
  waiting for transfers between devices: 215 us -> 133 us
  blocking collectives: 62.3 us -> 0 us
  other arithmetic: 100 us -> 38.1 us
  local copies, waits for them, and re-layouts: 239 us -> 182 us
    pallas_call x0 -> x1, Pallas kernels: none -> 120 us  [local_filter(): pl.pallas_call(functools.partial(local_filter_kernel, groups), grid=(tria...]
    psum x1 -> x0, waiting for transfers between devices: 98 us -> none  [from_root(): return lax.psum(block, axis)]
    dot_general x4 -> x1, matrix products: 148 us -> 57.7 us  [body(): jnp.einsum('rtk,ck->rtc', profile, operator, preferred_element_type=f32)]
    psum x1 -> x0, blocking collectives: 62.3 us -> none  [body(): totals = lax.psum((background, misfit), ('band', 'sector'))]
    ppermute x0 -> x13, waiting for transfers between devices: none -> 59 us  [the longest x6 35.4 us: shifted(): return lax.ppermute(x, axis, [(s, (s + shift) % n) for s in range(n)])]
    select_n x66 -> x2, other arithmetic: 44.7 us -> 0.1 us  [the longest x1 0.08 us: body(): jnp.where((source < me)[:, None], jnp.exp(log_b[None, :] * (lat_dev * pow...]
    all_gather x4 -> x1, waiting for transfers between devices: 79.2 us -> 40.6 us  [body(): band_ends = lax.all_gather(band_end, 'band')]
    slice x4 -> x5, local copies, waits for them, and re-layouts: 39.1 us -> 7.9 us  [the longest x1 5.92 us: body(): local[:, :, lat_dev - 1, :]]
  transfers between devices with their start and end apart: 9 -> 16, of which waited for: 6 -> 14; matrix products, arithmetic and copies ran while one was open for 53% -> 9% of each run, Pallas kernels for 0% -> 0%
where the time goes in v1:
time: 574 us; the launch traced here: 567 us
  local copies, waits for them, and re-layouts  182 us (32%)
  waiting for transfers between devices  133 us (23%)
  Pallas kernels  120 us (21%)
  matrix products  57.7 us (10%)
  other arithmetic  38.1 us (7%)
  starting transfers between devices  21 us (4%)
  between operations  14.8 us (3%)
    pallas_call x1, Pallas kernels, local_filter(): pl.pallas_call(functools.partial(local_filter_kernel, groups), grid=(tria...  120 us
    gather x4, local copies, waits for them, and re-layouts, body(): picked = table.at[where + offset].get(mode='promise_in_bounds')  80.6 us
    dot_general x1, matrix products, body(): jnp.einsum('rtk,ck->rtc', profile, operator, preferred_element_type=f32)  57.7 us
    unnamed x50, local copies, waits for them, and re-layouts  49.8 us
    all_gather x1, waiting for transfers between devices, body(): band_ends = lax.all_gather(band_end, 'band')  40.6 us
    ppermute x6, waiting for transfers between devices, shifted(): return lax.ppermute(x, axis, [(s, (s + shift) % n) for s in range(n)])  35.4 us
    reshape x1, local copies, waits for them, and re-layouts, body(): jnp.transpose(increment, (2, 3, 0, 1))  24.7 us
    ppermute x7, waiting for transfers between devices, xor_total(): x = x + lax.ppermute(x, axis, [(s, s ^ bit) for s in range(n)])  23.6 us
  transfers between devices with their start and end apart: 16, of which 14 were waited for; matrix products, arithmetic and copies ran while one was open for 9% of the time, Pallas kernels for 0%

profile of v1, /device:TPU:0, one launch (start us, length us, event | category | flops | bytes accessed | tf_op | source)
XLA Modules:
  0.0 567.5 jit_solution(16246813730878685773)
XLA Ops:
  7.2 3.3 pad.32
  10.6 3.1 copy.95
  14.1 3.0 copy.96
  17.2 1.1 pad.21.mix_ref
  18.3 3.5 add_convert_fusion
  21.8 6.5 %pad.22.x_ref = bf16[4,768,2048]{2,1,0:T(8,128)(2,1)} pad(bf16[4,762,2048]{2,1,0:T(8,128)(2,1)S(1)} %add_convert_fusion, bf16[]{:T(256)} %constant.10.clone.1), padding=0_0x0_6x0_0 | pad | bytes 25067522 | tf_op jit(solution)/shard_map/jit(_pad)/pad | solution.py:118
  29.0 0.9 broadcast_in_dim.24.lat_ref
  29.9 2.0 broadcast_in_dim.23.apow_ref
  31.9 120.1 %shard_map.131 = (f32[4,768,2048]{2,1,0:T(8,128)}, f32[4,768,128]{2,1,0:T(8,128)}) custom-call(bf16[768,768]{1,0:T(8,128)(2,1)} %pad.21.mix_ref, bf16[4,768,2048]{2,1,0:T(8,128)(2,1)} %pad.22.x_ref, f32[7,768,128]{2,1,0:T(8,128)} %broadcast_in_dim.23.apow_ref, f32[768,128]{1,0:T(8,128)} %broadcast_in_dim.24.lat_ref), custom_call_target="tpu_custom_call" | custom-call | flops 9852420096 | bytes 42467328 | tf_op jit(solution)/shard_map/pallas_call | solution.py:46
  152.0 1.8 copy.75
  153.8 1.7 collective-permute-start.1
  155.5 9.5 %collective-permute-done.1 = f32[4,768,16]{1,2,0:T(8,128)S(1)} collective-permute-done((f32[4,768,16]{1,2,0:T(8,128)S(1)}, f32[4,768,16]{1,2,0:T(8,128)S(1)}, u32[]{:S(2)}, u32[]{:S(2)}) %collective-permute-start.1) | collective-permute-done | bytes 196640 | tf_op jit(solution)/shard_map/ppermute | solution.py:72
  165.0 1.2 collective-permute-done
  166.3 9.0 %collective-permute-done.2 = f32[4,768,16]{1,2,0:T(8,128)S(1)} collective-permute-done((f32[4,768,16]{1,2,0:T(8,128)S(1)}, f32[4,768,16]{1,2,0:T(8,128)S(1)}, u32[]{:S(2)}, u32[]{:S(2)}) %collective-permute-start.2) | collective-permute-done | bytes 196640 | tf_op jit(solution)/shard_map/ppermute | solution.py:72
  175.4 9.4 %collective-permute-done.3 = f32[4,768,16]{1,2,0:T(8,128)S(1)} collective-permute-done((f32[4,768,16]{1,2,0:T(8,128)S(1)}, f32[4,768,16]{1,2,0:T(8,128)S(1)}, u32[]{:S(2)}, u32[]{:S(2)}) %collective-permute-start.3) | collective-permute-done | bytes 196640 | tf_op jit(solution)/shard_map/ppermute | solution.py:72
  184.9 21.3 %copy.97 = f32[384,8,16,128]{3,2,1,0:T(8,128)} copy(f32[384,8,16,128]{3,1,2,0:T(8,128)} %bitcast.61) | data formatting | bytes 50331648
  206.2 5.9 %slice.130 = f32[4,768,1,128]{3,2,1,0:T(1,128)S(1)} slice(f32[4,768,16,128]{3,2,1,0:T(8,128)} %bitcast.53), slice={[0:4], [0:768], [15:16], [0:128]} | slice | bytes 3145728 | tf_op jit(solution)/shard_map/slice | solution.py:157
  212.2 0.7 collective-permute-start.5
  213.1 6.4 %collective-permute-done.5 = f32[4,768,16]{1,2,0:T(8,128)S(1)} collective-permute-done((f32[4,768,16]{1,2,0:T(8,128)S(1)}, f32[4,768,16]{1,2,0:T(8,128)S(1)}, u32[]{:S(2)}, u32[]{:S(2)}) %collective-permute-start.5) | collective-permute-done | bytes 196640 | tf_op jit(solution)/shard_map/ppermute | solution.py:72
  219.7 1.7 add_multiply_fusion.1
  221.8 1.0 copy.72
  222.8 8.6 %all-to-all-start = ((f32[128,8,5]{1,2,0:T(8,128)}), f32[128,8,5]{1,2,0:T(8,128)S(1)}, u32[]{:S(2)}, u32[]{:S(2)}) async-start(f32[128,8,5]{1,2,0:T(8,128)} %copy.72), calls=%async_computation | async-start | bytes 1048576 | tf_op jit(solution)/shard_map/all_to_all | solution.py:113
  231.6 1.0 copy.78
  232.5 12.3 %all-to-all-done = f32[128,8,5]{1,2,0:T(8,128)S(1)} async-done(((f32[128,8,5]{1,2,0:T(8,128)}), f32[128,8,5]{1,2,0:T(8,128)S(1)}, u32[]{:S(2)}, u32[]{:S(2)}) %all-to-all-start) | async-done | bytes 20512 | tf_op jit(solution)/shard_map/all_to_all | solution.py:113
  246.3 0.7 copy.86
  247.1 0.7 copy.84
  247.8 0.7 copy.82
  251.6 40.6 %all-gather.2.cloned.1.call-done = f32[4,4,768,128]{3,2,1,0:T(8,128)} async-done(((f32[1,4,768,128]{3,2,1,0:T(8,128)}), f32[4,4,768,128]{3,2,1,0:T(8,128)}) %all-gather.2.cloned.1.call-update) | async-done | bytes 6291472 | tf_op jit(solution)/shard_map/all_gather | solution.py:159
  292.3 3.3 multiply_reduce_fusion.1
  295.5 15.6 %add_multiply_fusion = f32[4,768,16,128]{3,2,1,0:T(8,128)S(1)} fusion(f32[4,768,128]{2,1,0:T(8,128)S(1)} %multiply_reduce_fusion.1, f32[768,16]{1,0:T(8,128)} %copy.78, f32[4,768,16]{2,1,0:T(8,128)S(1)} %copy.77, f32[768,128]{1,0:T(8,128)S(1)} %multiply_exponential_fusion, f32[768]{0:T(1024)S(1)} %get-tuple-element.44, f32[768]{0:T(1024)} %get-tuple-element.55, ...), kind=kLoop, calls=%fused_computation.5 | loop fusion | flops 37748736 | bytes 52549632 | tf_op jit(solution)/shard_map/mul | solution.py:168
  311.1 15.9 %copy.132 = f32[384,8,16,128]{3,1,2,0:T(8,128)} copy(f32[384,8,16,128]{3,2,1,0:T(8,128)S(1)} %bitcast.55) | data formatting | bytes 50331648
  327.0 24.7 %copy.92 = f32[2048,3072]{1,0:T(8,128)} copy(f32[2048,3072]{0,1:T(8,128)} %bitcast.56) | data formatting | bytes 50331648 | tf_op jit(solution)/shard_map/reshape | solution.py:173
  351.8 20.2 %gather_fusion.3 = f32[1024,3072]{1,0:T(8,128)} fusion(f32[2048,3072]{1,0:T(8,128)} %copy.92, s32[1024]{0:T(1024)S(1)} %copy-done.11), kind=kCustom, calls=%fused_computation.3 | custom fusion | bytes 25169920 | tf_op jit(solution)/shard_map/gather | solution.py:179
  371.9 20.1 %gather_fusion.2 = f32[1024,3072]{1,0:T(8,128)} fusion(f32[2048,3072]{1,0:T(8,128)} %copy.92, s32[1024]{0:T(1024)S(1)} %copy-done.10), kind=kCustom, calls=%fused_computation.2 | custom fusion | bytes 25169920 | tf_op jit(solution)/shard_map/gather | solution.py:179
  392.1 20.1 %gather_fusion.1 = f32[1024,3072]{1,0:T(8,128)} fusion(f32[2048,3072]{1,0:T(8,128)} %copy.92, s32[1024]{0:T(1024)S(1)} %copy-done.9), kind=kCustom, calls=%fused_computation.1 | custom fusion | bytes 25169920 | tf_op jit(solution)/shard_map/gather | solution.py:179
  412.2 20.2 %gather_fusion = f32[1024,3072]{1,0:T(8,128)} fusion(f32[2048,3072]{1,0:T(8,128)} %copy.92, s32[1024]{0:T(1024)S(1)} %copy-done.8), kind=kCustom, calls=%fused_computation | custom fusion | bytes 25169920 | tf_op jit(solution)/shard_map/gather | solution.py:179
  432.5 57.7 %fusion.4 = f32[128,8,4,128]{3,0,2,1:T(8,128)S(1)} fusion(f32[128,8,4,768]{3,1,2,0:T(8,128)} %bitcast.57, f32[128,8,4,768]{3,1,2,0:T(8,128)} %bitcast.58, f32[128,8,4,768]{3,1,2,0:T(8,128)} %bitcast.59, f32[128,8,4,768]{3,1,2,0:T(8,128)} %bitcast.60, f32[128,8]{0,1:T(8,128)S(1)} %copy-done.4, f32[128,8]{0,1:T(8,128)S(1)} %copy-done.5, ...), kind=kOutput, calls=%fused_computation.17 | convolution fusion | flops 830472192 | bytes 52640256 | tf_op jit(solution)/shard_map/rtk,ck->rtc/dot_general | solution.py:184
  490.2 2.7 copy.88
  492.9 7.2 %all-to-all-start.1 = ((f32[128,8,4,128]{3,2,1,0:T(4,128)}), f32[128,8,4,128]{3,2,1,0:T(4,128)S(1)}, u32[]{:S(2)}, u32[]{:S(2)}) async-start(f32[128,8,4,128]{3,2,1,0:T(4,128)} %copy.88), calls=%async_computation.1 | async-start | bytes 4194304 | tf_op jit(solution)/shard_map/all_to_all | solution.py:187
  500.2 9.0 %multiply_reduce_fusion = f32[4]{0:T(128)S(1)} fusion(f32[762,16,128]{2,1,0:T(8,128)} %param.13, f32[4]{0:T(128)S(1)} %copy-done.17, f32[762,16,128]{2,1,0:T(8,128)} %param.12), kind=kLoop, calls=%fused_computation.7 | loop fusion | flops 24969212 | bytes 12484640 | tf_op jit(solution)/shard_map/reduce_sum | solution.py:116
  509.2 21.3 %all-to-all-done.1 = f32[128,8,4,128]{3,2,1,0:T(4,128)S(1)} async-done(((f32[128,8,4,128]{3,2,1,0:T(4,128)}), f32[128,8,4,128]{3,2,1,0:T(4,128)S(1)}, u32[]{:S(2)}, u32[]{:S(2)}) %all-to-all-start.1) | async-done | bytes 2097184 | tf_op jit(solution)/shard_map/all_to_all | solution.py:187
  531.1 2.7 copy.90
  534.4 3.0 collective-permute-done.7
  538.1 4.5 collective-permute-done.8
  542.8 3.4 collective-permute-done.9
  546.4 4.8 collective-permute-done.10
  551.6 3.2 collective-permute-done.11
  555.2 4.7 collective-permute-done.12
  (109 shorter events, 11.0 us)
Async XLA Ops:
  7.2 6.5 %slice-start = ((s8[6242304]{0:T(1024)(128)(4,1)}), s8[2048000]{0:T(1024)(128)(4,1)S(1)}, s32[]{:S(2)}) async-start(s8[6242304]{0:T(1024)(128)(4,1)} %bitcast.66), calls=%async_computation.3 | async-start | bytes 4096000
  7.2 285.1 %all-gather.2.cloned.1.call-start = ((), (), s32[]{:S(2)}) async-start(), calls=%async_computation.2 | async-start | bytes 7864320 | tf_op jit(solution)/shard_map/all_gather | solution.py:159
  10.5 3.1 slice-start.1
  13.7 3.5 copy-start
  13.7 4.6 copy-start.16
  21.8 6.5 %copy-start.13 = (f32[762]{0:T(1024)S(1)}, f32[762]{0:T(1024)}, u32[]{:S(2)}) copy-start(f32[762]{0:T(1024)} %param.16) | copy-start | bytes 9148
  21.8 6.5 %copy-start.14 = (f32[762]{0:T(1024)S(1)}, f32[762]{0:T(1024)}, u32[]{:S(2)}) copy-start(f32[762]{0:T(1024)} %param.17) | copy-start | bytes 9148
  153.8 11.1 %collective-permute-start.1 = (f32[4,768,16]{1,2,0:T(8,128)S(1)}, f32[4,768,16]{1,2,0:T(8,128)S(1)}, u32[]{:S(2)}, u32[]{:S(2)}) collective-permute-start(f32[4,768,16]{1,2,0:T(8,128)S(1)} %copy.75), channel_id=1, source_target_pairs={{0,2},{1,3},{2,4},{3,5},{4,6},{5,7},{6,8},{7,9},{8,10},{9,11},{10,... | collective-permute-start | bytes 589832 | tf_op jit(solution)/shard_map/ppermute | solution.py:72
  155.5 10.7 %collective-permute-start = (f32[4,768,16]{1,2,0:T(8,128)S(1)}, f32[4,768,16]{1,2,0:T(8,128)S(1)}, u32[]{:S(2)}, u32[]{:S(2)}) collective-permute-start(f32[4,768,16]{1,2,0:T(8,128)S(1)} %copy.75), channel_id=1, source_target_pairs={{0,1},{1,2},{2,3},{3,4},{4,5},{5,6},{6,7},{7,8},{8,9},{9,10},{10,1... | collective-permute-start | bytes 589832 | tf_op jit(solution)/shard_map/ppermute | solution.py:72
  166.2 9.1 %collective-permute-start.2 = (f32[4,768,16]{1,2,0:T(8,128)S(1)}, f32[4,768,16]{1,2,0:T(8,128)S(1)}, u32[]{:S(2)}, u32[]{:S(2)}) collective-permute-start(f32[4,768,16]{1,2,0:T(8,128)S(1)} %multiply_add_fusion.3), channel_id=1, source_target_pairs={{0,2},{1,3},{2,4},{3,5},{4,6},{5,7},{6,8},{7,9},{8,10},{9,11},{10,... | collective-permute-start | bytes 589832 | tf_op jit(solution)/shard_map/ppermute | solution.py:72
  175.3 9.5 %collective-permute-start.3 = (f32[4,768,16]{1,2,0:T(8,128)S(1)}, f32[4,768,16]{1,2,0:T(8,128)S(1)}, u32[]{:S(2)}, u32[]{:S(2)}) collective-permute-start(f32[4,768,16]{1,2,0:T(8,128)S(1)} %multiply_add_fusion.2), channel_id=1, source_target_pairs={{0,4},{1,5},{2,6},{3,7},{4,8},{5,9},{6,10},{7,11},{8,12},{9,13},{1... | collective-permute-start | bytes 589832 | tf_op jit(solution)/shard_map/ppermute | solution.py:72
  184.8 27.3 %collective-permute-start.4 = (f32[4,768,16]{1,2,0:T(8,128)S(1)}, f32[4,768,16]{1,2,0:T(8,128)S(1)}, u32[]{:S(2)}, u32[]{:S(2)}) collective-permute-start(f32[4,768,16]{1,2,0:T(8,128)S(1)} %multiply_add_fusion.1), channel_id=1, source_target_pairs={{0,8},{1,9},{2,10},{3,11},{4,12},{5,13},{6,14},{7,15},{8,16},{9,17... | collective-permute-start | bytes 589832 | tf_op jit(solution)/shard_map/ppermute | solution.py:72
  184.9 36.6 %copy-start.15 = (s32[1024]{0:T(1024)S(1)}, s32[1024]{0:T(1024)}, u32[]{:S(2)}) copy-start(s32[1024]{0:T(1024)} %param.21) | copy-start | bytes 12292
  184.9 36.7 %copy-start.12 = (f32[1024,4]{0,1:T(4,128)S(1)}, f32[1024,4]{0,1:T(4,128)}, u32[]{:S(2)}) copy-start(f32[1024,4]{0,1:T(4,128)} %param.22) | copy-start | bytes 49156
  212.2 7.3 %collective-permute-start.5 = (f32[4,768,16]{1,2,0:T(8,128)S(1)}, f32[4,768,16]{1,2,0:T(8,128)S(1)}, u32[]{:S(2)}, u32[]{:S(2)}) collective-permute-start(f32[4,768,16]{1,2,0:T(8,128)S(1)} %multiply_add_fusion), channel_id=1, source_target_pairs={{0,16},{1,17},{2,18},{3,19},{4,20},{5,21},{6,22},{7,23},{8,24},{9,... | collective-permute-start | bytes 589832 | tf_op jit(solution)/shard_map/ppermute | solution.py:72
  222.8 22.1 %all-to-all-start = ((f32[128,8,5]{1,2,0:T(8,128)}), f32[128,8,5]{1,2,0:T(8,128)S(1)}, u32[]{:S(2)}, u32[]{:S(2)}) async-start(f32[128,8,5]{1,2,0:T(8,128)} %copy.72), calls=%async_computation | async-start | bytes 1048576 | tf_op jit(solution)/shard_map/all_to_all | solution.py:113
  327.0 24.7 %copy-start.11 = (s32[1024]{0:T(1024)S(1)}, s32[1024]{0:T(1024)}, u32[]{:S(2)}) copy-start(s32[1024]{0:T(1024)} %broadcast_clamp_fusion) | copy-start | bytes 12292
  351.8 20.2 %copy-start.10 = (s32[1024]{0:T(1024)S(1)}, s32[1024]{0:T(1024)}, u32[]{:S(2)}) copy-start(s32[1024]{0:T(1024)} %broadcast_clamp_fusion.1) | copy-start | bytes 12292
  371.9 20.1 %copy-start.9 = (s32[1024]{0:T(1024)S(1)}, s32[1024]{0:T(1024)}, u32[]{:S(2)}) copy-start(s32[1024]{0:T(1024)} %broadcast_clamp_fusion.2) | copy-start | bytes 12292
  392.1 20.1 %copy-start.8 = (s32[1024]{0:T(1024)S(1)}, s32[1024]{0:T(1024)}, u32[]{:S(2)}) copy-start(s32[1024]{0:T(1024)} %broadcast_clamp_fusion.3) | copy-start | bytes 12292
  412.2 20.2 %copy-start.3 = (f32[128,8]{0,1:T(8,128)S(1)}, f32[128,8]{0,1:T(8,128)}, u32[]{:S(2)}) copy-start(f32[128,8]{0,1:T(8,128)} %copy.74) | copy-start | bytes 12292
  412.2 20.2 %copy-start.4 = (f32[128,8]{0,1:T(8,128)S(1)}, f32[128,8]{0,1:T(8,128)}, u32[]{:S(2)}) copy-start(f32[128,8]{0,1:T(8,128)} %copy.86) | copy-start | bytes 12292
  412.2 20.2 %copy-start.5 = (f32[128,8]{0,1:T(8,128)S(1)}, f32[128,8]{0,1:T(8,128)}, u32[]{:S(2)}) copy-start(f32[128,8]{0,1:T(8,128)} %copy.84) | copy-start | bytes 12292
  412.2 20.2 %copy-start.6 = (f32[128,8]{0,1:T(8,128)S(1)}, f32[128,8]{0,1:T(8,128)}, u32[]{:S(2)}) copy-start(f32[128,8]{0,1:T(8,128)} %copy.82) | copy-start | bytes 12292
  412.2 20.2 %copy-start.7 = (bf16[128,762]{1,0:T(8,128)(2,1)S(1)}, bf16[128,762]{1,0:T(8,128)(2,1)}, u32[]{:S(2)}) copy-start(bf16[128,762]{1,0:T(8,128)(2,1)} %param.18) | copy-start | bytes 585220
  432.5 67.6 %copy-start.18 = (s32[1,128]{1,0:T(1,128)S(1)}, s32[1,128]{1,0:T(1,128)}, u32[]{:S(2)}) copy-start(s32[1,128]{1,0:T(1,128)} %param.23) | copy-start | bytes 1540
  432.5 67.7 %copy-start.17 = (f32[4]{0:T(128)S(1)}, f32[4]{0:T(128)}, u32[]{:S(2)}) copy-start(f32[4]{0:T(128)} %param.14) | copy-start | bytes 52
  490.2 40.2 %copy-start.1 = (f32[1024,128]{1,0:T(8,128)S(1)}, f32[1024,128]{1,0:T(8,128)}, u32[]{:S(2)}) copy-start(f32[1024,128]{1,0:T(8,128)} %param.20) | copy-start | bytes 1572868
  490.2 40.2 %copy-start.2 = (f32[1024,128]{1,0:T(8,128)S(1)}, f32[1024,128]{1,0:T(8,128)}, u32[]{:S(2)}) copy-start(f32[1024,128]{1,0:T(8,128)} %param.19) | copy-start | bytes 1572868
  492.9 37.5 %all-to-all-start.1 = ((f32[128,8,4,128]{3,2,1,0:T(4,128)}), f32[128,8,4,128]{3,2,1,0:T(4,128)S(1)}, u32[]{:S(2)}, u32[]{:S(2)}) async-start(f32[128,8,4,128]{3,2,1,0:T(4,128)} %copy.88), calls=%async_computation.1 | async-start | bytes 4194304 | tf_op jit(solution)/shard_map/all_to_all | solution.py:187
  531.0 2.8 collective-permute-start.6
  533.7 3.7 collective-permute-start.7
  537.4 5.2 collective-permute-start.8
  542.6 3.6 collective-permute-start.9
  546.2 5.1 collective-permute-start.10
  551.2 3.6 collective-permute-start.11
  554.8 5.1 collective-permute-start.12
Sparse Core Ops, SparseCore 0:
  221.6 70.6 all-gather.1

commit v2 on v1

v2 whole, which is shorter than its diff:
```python
import functools

import jax
import jax.numpy as jnp
from jax import lax
from jax.experimental import pallas as pl
from jax.experimental.pallas import tpu as pltpu
from jax.sharding import PartitionSpec as P

LANES = 128
LINE_TILE = 256


def padded_lines(n):
    return -(-n // LINE_TILE) * LINE_TILE


def local_filter_kernel(lat_dev, lon_dev, x_ref, mix_ref, a_ref, b_ref, out_ref, end_ref):
    chunks, rows, _ = out_ref.shape
    block = 256

    def mix_rows(c, carry):
        at = pl.ds(pl.multiple_of(c * block, block), block)
        res = jnp.dot(x_ref[at, :], mix_ref[...], preferred_element_type=jnp.float32)
        for lc in range(chunks):
            out_ref[lc, at, :] = res[:, lc * LANES:(lc + 1) * LANES]
        return carry

    lax.fori_loop(0, rows // block, mix_rows, 0)

    def lon_step(j, states):
        at = pl.ds(j, lat_dev, stride=lon_dev)
        new = []
        for lc in range(chunks):
            state = a_ref[lc] * states[lc] + out_ref[lc, at, :]
            out_ref[lc, at, :] = state
            new.append(state)
        return tuple(new)

    zero = jnp.zeros((lat_dev, LANES), jnp.float32)
    ends = lax.fori_loop(0, lon_dev, lon_step, (zero,) * chunks)
    for lc in range(chunks):
        end_ref[lc] = ends[lc]

    for lc in range(chunks):
        def lat_step(i, state, lc=lc):
            at = pl.ds(pl.multiple_of(i * lon_dev, lon_dev), lon_dev)
            state = b_ref[lc] * state + out_ref[lc, at, :]
            out_ref[lc, at, :] = state
            return state

        lax.fori_loop(1, lat_dev, lat_step, out_ref[lc, pl.ds(0, lon_dev), :])


def local_filter(xt, mix, a_rows, b_rows, lat_dev, lon_dev):
    trials, positions, klen = xt.shape
    kpad = mix.shape[1]
    chunks = kpad // LANES
    flops = 2 * positions * klen * kpad * trials + 4 * trials * positions * kpad
    bytes_accessed = xt.size * 2 + trials * positions * kpad * 4 + mix.size * 2
    return pl.pallas_call(
        functools.partial(local_filter_kernel, lat_dev, lon_dev),
        grid=(trials,),
        in_specs=[
            pl.BlockSpec((None, positions, klen), lambda t: (t, 0, 0)),
            pl.BlockSpec((klen, kpad), lambda t: (0, 0)),
            pl.BlockSpec((chunks, lat_dev, LANES), lambda t: (0, 0, 0)),
            pl.BlockSpec((chunks, lon_dev, LANES), lambda t: (0, 0, 0)),
        ],
        out_specs=[
            pl.BlockSpec((None, chunks, positions, LANES), lambda t: (t, 0, 0, 0)),
            pl.BlockSpec((None, chunks, lat_dev, LANES), lambda t: (t, 0, 0, 0)),
        ],
        out_shape=[
            jax.ShapeDtypeStruct((trials, chunks, positions, LANES), jnp.float32),
            jax.ShapeDtypeStruct((trials, chunks, lat_dev, LANES), jnp.float32),
        ],
        compiler_params=pltpu.CompilerParams(
            dimension_semantics=("arbitrary",), vmem_limit_bytes=48 * 1024 * 1024
        ),
        cost_estimate=pl.CostEstimate(
            flops=flops, bytes_accessed=bytes_accessed, transcendentals=0
        ),
    )(xt, mix, a_rows, b_rows)


def shifted(x, axis, shift):
    n = lax.axis_size(axis)
    return lax.ppermute(x, axis, [(s, (s + shift) % n) for s in range(n)])


def xor_total(x, axes):
    for axis in axes:
        n = lax.axis_size(axis)
        bit = 1
        while bit < n:
            x = x + lax.ppermute(x, axis, [(s, s ^ bit) for s in range(n)])
            bit *= 2
    return x


def body(
    control,
    direction,
    step_lengths,
    level_root,
    lon_decay,
    lat_decay,
    obs_operator,
    obs_values,
    obs_inv_err,
    obs_cols,
    obs_weights,
    counts,
):
    num_lines, lat_dev, lon_dev = control.shape
    trials = step_lengths.shape[0]
    channels = obs_values.shape[1]
    bands = lax.axis_size("band")
    sectors = lax.axis_size("sector")
    devices_all = bands * sectors
    capacity = obs_cols.shape[0] // devices_all
    kpad = padded_lines(num_lines)
    extra = kpad - num_lines
    f32 = jnp.float32

    packed = jnp.concatenate(
        [obs_cols.astype(f32)[:, None], obs_weights], axis=1
    ).reshape(devices_all, capacity, 5)
    packed = lax.all_to_all(packed, ("band", "sector"), 0, 0, tiled=True)

    trial_fields = control[None] + step_lengths[:, None, None, None] * direction[None]
    background = jnp.sum(trial_fields * trial_fields, axis=(1, 2, 3))
    xt = trial_fields.astype(jnp.bfloat16).reshape(trials, num_lines, lat_dev * lon_dev)
    xt = jnp.pad(jnp.transpose(xt, (0, 2, 1)), ((0, 0), (0, 0), (0, extra)))
    mix_t = jnp.pad(level_root, ((0, extra), (0, extra))).T

    a = jnp.pad(lon_decay, (0, extra), constant_values=0.5)
    b = jnp.pad(lat_decay, (0, extra), constant_values=0.5)
    chunks = kpad // LANES

    def by_chunk(v):
        v = v.reshape(v.shape[:-1] + (chunks, LANES))
        return jnp.moveaxis(v, -2, 0)

    a_c = by_chunk(a)
    b_c = by_chunk(b)
    log_a_c = jnp.log(a_c)
    log_b_c = jnp.log(b_c)
    a_rows = jnp.broadcast_to(a_c[:, None, :], (chunks, lat_dev, LANES))
    b_rows = jnp.broadcast_to(b_c[:, None, :], (chunks, lon_dev, LANES))

    local, lon_ends = local_filter(xt, mix_t, a_rows, b_rows, lat_dev, lon_dev)
    local = local.reshape(trials, chunks, lat_dev, lon_dev, LANES)

    per_line = lambda v: v[None, :, None, :]
    carried = shifted(lon_ends, "sector", 1)
    carried = carried + per_line(jnp.exp(log_a_c * lon_dev)) * shifted(lon_ends, "sector", 2)
    span = 2
    while span < sectors:
        gain = jnp.exp(log_a_c * (lon_dev * span))
        carried = carried + per_line(gain) * shifted(carried, "sector", span)
        span *= 2
    loop_gain = 1.0 - jnp.exp(log_a_c * (lon_dev * sectors))
    incoming = carried / per_line(loop_gain)

    rows = []
    state = jnp.zeros((trials, chunks, LANES), f32)
    for i in range(lat_dev):
        state = b_c[None] * state + incoming[:, :, i, :]
        rows.append(state)
    incoming_lat = jnp.stack(rows, axis=2)
    lon_rise = jnp.exp(log_a_c[:, None, :] * jnp.arange(1, lon_dev + 1).astype(f32)[None, :, None])
    lat_rise = jnp.exp(log_b_c[:, None, :] * jnp.arange(1, lat_dev + 1).astype(f32)[None, :, None])
    scale_a = jnp.sqrt(1.0 - a_c * a_c)[:, None, :]
    scale_b = jnp.sqrt(1.0 - b_c * b_c)[:, None, None, :]

    band_end = scale_a * (
        local[:, :, lat_dev - 1] + lon_rise[None] * incoming_lat[:, :, lat_dev - 1, None, :]
    )
    band_ends = lax.all_gather(band_end, "band")
    me = lax.axis_index("band")
    source = jnp.arange(bands)
    power = (me - 1 - source).astype(f32)
    band_weight = jnp.where(
        (source < me)[:, None, None],
        jnp.exp(log_b_c[None] * (lat_dev * power)[:, None, None]),
        0.0,
    )
    entering = jnp.sum(band_weight[:, None, :, None, :] * band_ends, axis=0)

    increment = scale_b * (
        scale_a[:, None] * (local + lon_rise[None, :, None] * incoming_lat[:, :, :, None, :])
        + lat_rise[None, :, :, None, :] * entering[:, :, None, :, :]
    )
    increment = increment.reshape(trials, chunks, lat_dev * lon_dev, LANES)

    where = packed[:, :, 0].astype(jnp.int32).reshape(-1, 1)
    weights = packed[:, :, 1:].reshape(-1, 4)
    position = jnp.arange(lat_dev * lon_dev, dtype=jnp.int32)[None, :]
    interp = None
    for corner, offset in enumerate((0, 1, lon_dev, lon_dev + 1)):
        term = jnp.where(position == where + offset, weights[:, corner, None], 0.0)
        interp = term if interp is None else interp + term
    profile = jnp.einsum(
        "rp,tcpk->trck", interp, increment, precision=lax.Precision.HIGH,
        preferred_element_type=f32,
    ).astype(jnp.bfloat16)
    operator = jnp.pad(obs_operator, ((0, 0), (0, extra))).reshape(channels, chunks, LANES)
    evolved = jnp.einsum(
        "trck,ock->rto", profile, operator, preferred_element_type=f32
    ).reshape(devices_all, capacity, trials, channels)
    returned = lax.all_to_all(evolved, ("band", "sector"), 0, 0, tiled=True)

    observed = obs_values.reshape(devices_all, capacity, 1, channels)
    inverse = obs_inv_err.reshape(devices_all, capacity, 1, channels)
    live = counts[0][:, None] > jnp.arange(capacity, dtype=jnp.int32)[None, :]
    weighted = (returned - observed) * inverse
    departures = jnp.where(live[:, :, None, None], weighted, 0.0)
    misfit = jnp.sum(departures * departures, axis=(0, 1, 3))

    totals = xor_total(jnp.stack([background, misfit]), ("sector", "band"))
    cell_count = num_lines * lat_dev * lon_dev * devices_all
    cost_values = 0.5 * (totals[0] + totals[1]) / cell_count
    return (departures.reshape(devices_all * capacity, trials, channels), cost_values)


def solution(mesh):
    placed = (
        P(None, "band", "sector"),
        P(None, "band", "sector"),
        P(),
        P(),
        P(),
        P(),
        P(),
        P(("band", "sector"), None),
        P(("band", "sector"), None),
        P(("band", "sector")),
        P(("band", "sector"), None),
        P(("band", "sector"), None),
    )
    return jax.shard_map(
        body,
        mesh=mesh,
        in_specs=placed,
        out_specs=(P(("band", "sector"), None, None), P()),
        check_vma=False,
    )
```

time: 574 us -> 430 us (0.75)
  local copies, waits for them, and re-layouts: 182 us -> 30.9 us
  Pallas kernels: 120 us -> 73.5 us
  matrix products: 57.7 us -> 95.3 us
  other arithmetic: 38.1 us -> 51.2 us
  waiting for transfers between devices: 133 us -> 143 us
    gather x4 -> x0, local copies, waits for them, and re-layouts: 80.6 us -> none  [body(): picked = table.at[where + offset].get(mode='promise_in_bounds')]
    pallas_call x1, Pallas kernels: 120 us -> 73.5 us  [local_filter(): pl.pallas_call(functools.partial(local_filter_kernel, lat_dev, lon_dev),...]
    unnamed x50 -> x27, local copies, waits for them, and re-layouts: 49.8 us -> 3.51 us
    dot_general x1 -> x2, matrix products: 57.7 us -> 95.3 us  [the longest x1 90.2 us: body(): jnp.einsum('rp,tcpk->trck', interp, increment, precision=lax.Precision.HI...]
    reshape x1 -> x3, local copies, waits for them, and re-layouts: 24.7 us -> 2.31 us  [the longest x1 1.61 us: body(): evolved = jnp.einsum('trck,ock->rto', profile, operator, preferred_elemen...]
    ppermute x6, waiting for transfers between devices: 35.4 us -> 45 us  [shifted(): return lax.ppermute(x, axis, [(s, (s + shift) % n) for s in range(n)])]
    slice x3 -> x1, local copies, waits for them, and re-layouts: 7.81 us -> 0.01 us  [body(): term = jnp.where(position == where + offset, weights[:, corner, None], 0.0)]
    add x0 -> x2, local copies, waits for them, and re-layouts: none -> 6.62 us  [the longest x1 6.62 us: body(): control[None] + step_lengths[:, None, None, None] * direction[None]]
  transfers between devices with their start and end apart: 16 -> 16, of which waited for: 14 -> 15; matrix products, arithmetic and copies ran while one was open for 9% -> 5% of each run, Pallas kernels for 0% -> 0%
where the time goes in v2:
time: 430 us; the launch traced here: 427 us
  waiting for transfers between devices  143 us (33%)
  matrix products  95.3 us (22%)
  Pallas kernels  73.5 us (17%)
  other arithmetic  51.2 us (12%)
  local copies, waits for them, and re-layouts  30.9 us (7%)
  starting transfers between devices  18.4 us (4%)
  between operations  14.6 us (3%)
    dot_general x1, matrix products, body(): jnp.einsum('rp,tcpk->trck', interp, increment, precision=lax.Precision.HI...  90.2 us
    pallas_call x1, Pallas kernels, local_filter(): pl.pallas_call(functools.partial(local_filter_kernel, lat_dev, lon_dev),...  73.5 us
    ppermute x6, waiting for transfers between devices, shifted(): return lax.ppermute(x, axis, [(s, (s + shift) % n) for s in range(n)])  45 us
    all_gather x1, waiting for transfers between devices, body(): band_ends = lax.all_gather(band_end, 'band')  39.9 us
    ppermute x7, waiting for transfers between devices, xor_total(): x = x + lax.ppermute(x, axis, [(s, s ^ bit) for s in range(n)])  23.6 us
    all_to_all x1, waiting for transfers between devices, body(): returned = lax.all_to_all(evolved, ('band', 'sector'), 0, 0, tiled=True)  21.3 us
    mul x1, other arithmetic, body(): scale_b * (scale_a[:, None] * (local + lon_rise[None, :, None] * incoming...  19.9 us
    all_to_all x1, waiting for transfers between devices, body(): packed = lax.all_to_all(packed, ('band', 'sector'), 0, 0, tiled=True)  13.1 us
  transfers between devices with their start and end apart: 16, of which 15 were waited for; matrix products, arithmetic and copies ran while one was open for 5% of the time, Pallas kernels for 0%

profile of v2, /device:TPU:0, one launch (start us, length us, event | category | flops | bytes accessed | tf_op | source)
XLA Modules:
  0.0 426.8 jit_solution(17581777091213537227)
XLA Ops:
  7.2 0.7 pad_bitcast_fusion.2
  7.9 6.6 %copy.101 = f32[762,16,128]{0,2,1:T(8,128)} copy(f32[762,16,128]{2,1,0:T(8,128)} %param.12) | data formatting | bytes 12484608 | tf_op jit(solution)/shard_map/add | solution.py:132
  14.5 6.7 %copy.102 = f32[762,16,128]{0,2,1:T(8,128)} copy(f32[762,16,128]{2,1,0:T(8,128)} %param.13) | data formatting | bytes 12484608 | tf_op jit(solution)/shard_map/mul | solution.py:132
  21.3 0.6 copy.82
  22.0 7.2 %add_convert_fusion = bf16[4,2048,762]{2,1,0:T(8,128)(2,1)S(1)} fusion(f32[2048,762]{1,0:T(8,128)} %bitcast.109, f32[4]{0:T(128)S(1)} %copy-done.8, f32[2048,762]{1,0:T(8,128)} %bitcast.108), kind=kLoop, calls=%fused_computation.6 | loop fusion | flops 18726912 | bytes 24969232 | tf_op jit(solution)/shard_map/convert_element_type | solution.py:134
  29.2 6.5 %pad.22.x_ref = bf16[4,2048,768]{2,1,0:T(8,128)(2,1)} pad(bf16[4,2048,762]{2,1,0:T(8,128)(2,1)S(1)} %add_convert_fusion, bf16[]{:T(256)} %constant.18.clone.1), padding=0_0x0_0x0_6 | pad | bytes 25067522 | tf_op jit(solution)/shard_map/jit(_pad)/pad | solution.py:135
  35.8 73.5 %shard_map.131 = (f32[4,6,2048,128]{3,2,1,0:T(8,128)}, f32[4,6,16,128]{3,2,1,0:T(8,128)S(1)}) custom-call(bf16[4,2048,768]{2,1,0:T(8,128)(2,1)} %pad.22.x_ref, bf16[768,768]{1,0:T(8,128)(2,1)S(1)} %pad_bitcast_fusion.mix_ref, f32[6,16,128]{2,1,0:T(8,128)S(1)} %broadcast_in_dim.102.a_ref, f32[6,128,128]{2,1,0:T(8,128)S(1)} %broadcast_in_dim.103.b_ref), custom_call_target="tpu_custom_call" | custom-call | flops 9688842240 | bytes 38928384 | tf_op jit(solution)/shard_map/pallas_call | solution.py:61
  109.4 1.7 collective-permute-start.1
  111.1 8.2 %collective-permute-done = f32[4,6,16,128]{3,2,1,0:T(8,128)S(1)} collective-permute-done((f32[4,6,16,128]{3,2,1,0:T(8,128)S(1)}, f32[4,6,16,128]{3,2,1,0:T(8,128)S(1)}, u32[]{:S(2)}, u32[]{:S(2)}) %collective-permute-start) | collective-permute-done | bytes 196640 | tf_op jit(solution)/shard_map/ppermute | solution.py:89
  119.2 1.3 collective-permute-done.1
  120.6 10.8 %collective-permute-done.2 = f32[4,6,16,128]{3,2,1,0:T(8,128)S(1)} collective-permute-done((f32[4,6,16,128]{3,2,1,0:T(8,128)S(1)}, f32[4,6,16,128]{3,2,1,0:T(8,128)S(1)}, u32[]{:S(2)}, u32[]{:S(2)}) %collective-permute-start.2) | collective-permute-done | bytes 196640 | tf_op jit(solution)/shard_map/ppermute | solution.py:89
  131.5 10.5 %collective-permute-done.3 = f32[4,6,16,128]{3,2,1,0:T(8,128)S(1)} collective-permute-done((f32[4,6,16,128]{3,2,1,0:T(8,128)S(1)}, f32[4,6,16,128]{3,2,1,0:T(8,128)S(1)}, u32[]{:S(2)}, u32[]{:S(2)}) %collective-permute-start.3) | collective-permute-done | bytes 196640 | tf_op jit(solution)/shard_map/ppermute | solution.py:89
  142.2 7.2 %collective-permute-done.4 = f32[4,6,16,128]{3,2,1,0:T(8,128)S(1)} collective-permute-done((f32[4,6,16,128]{3,2,1,0:T(8,128)S(1)}, f32[4,6,16,128]{3,2,1,0:T(8,128)S(1)}, u32[]{:S(2)}, u32[]{:S(2)}) %collective-permute-start.4) | collective-permute-done | bytes 196640 | tf_op jit(solution)/shard_map/ppermute | solution.py:89
  149.7 7.0 %collective-permute-done.5 = f32[4,6,16,128]{3,2,1,0:T(8,128)S(1)} collective-permute-done((f32[4,6,16,128]{3,2,1,0:T(8,128)S(1)}, f32[4,6,16,128]{3,2,1,0:T(8,128)S(1)}, u32[]{:S(2)}, u32[]{:S(2)}) %collective-permute-start.5) | collective-permute-done | bytes 196640 | tf_op jit(solution)/shard_map/ppermute | solution.py:89
  156.8 0.2 slice_add_fusion
  157.0 2.8 fusion.32
  160.2 1.0 copy.86
  161.2 6.3 %all-to-all-start = ((f32[128,8,5]{1,2,0:T(8,128)}), f32[128,8,5]{1,2,0:T(8,128)S(1)}, u32[]{:S(2)}, u32[]{:S(2)}) async-start(f32[128,8,5]{1,2,0:T(8,128)} %copy.86), calls=%async_computation | async-start | bytes 1048576 | tf_op jit(solution)/shard_map/all_to_all | solution.py:130
  167.9 13.1 %all-to-all-done = f32[128,8,5]{1,2,0:T(8,128)S(1)} async-done(((f32[128,8,5]{1,2,0:T(8,128)}), f32[128,8,5]{1,2,0:T(8,128)S(1)}, u32[]{:S(2)}, u32[]{:S(2)}) %all-to-all-start) | async-done | bytes 20512 | tf_op jit(solution)/shard_map/all_to_all | solution.py:130
  181.3 0.2 fusion.33
  181.6 6.5 %fusion.45 = f32[1024,2048,1,1]{1,0,3,2:T(8,128)} fusion(f32[1024]{0:T(1024)S(1)} %bitcast.118, s32[1024]{0:T(1024)S(1)} %get-tuple-element.37, f32[1024]{0:T(1024)S(1)} %bitcast.119, s32[1024]{0:T(1024)S(1)} %get-tuple-element.38, f32[1024]{0:T(1024)S(1)} %bitcast.120, s32[1024]{0:T(1024)S(1)} %get-tuple-element.36, f32[1024]{0:T(1024)S(1)} %bitcast.117, ...), kind=kLoop, calls=%fused_computation.9.clone.1 | loop fusion | flops 23068672 | bytes 8421376 | tf_op jit(solution)/shard_map/rp,tcpk->trck/dot_general | solution.py:205
  188.1 0.3 stack.8
  188.4 39.9 %all-gather.2.cloned.1.call-done = f32[4,4,6,128,128]{4,3,2,1,0:T(8,128)} async-done(((f32[1,4,6,128,128]{4,3,2,1,0:T(8,128)}), f32[4,4,6,128,128]{4,3,2,1,0:T(8,128)}) %all-gather.2.cloned.1.call-update) | async-done | bytes 6291472 | tf_op jit(solution)/shard_map/all_gather | solution.py:181
  228.3 3.8 multiply_reduce_fusion.1
  232.1 0.8 mul.558
  232.9 0.4 mul.608
  233.3 19.9 %fusion.1 = f32[4,6,2048,128]{3,2,1,0:T(8,128)} fusion(f32[4,6,2048,128]{3,2,1,0:T(8,128)} %get-tuple-element.4, f32[4,6,128,128]{3,2,1,0:T(8,128)S(1)} %multiply_reduce_fusion.1, f32[6,2048,128]{2,1,0:T(8,128)S(1)} %bitcast.107, f32[4,6,16,128]{3,2,1,0:T(8,128)S(1)} %stack.8, f32[6,2048,128]{2,1,0:T(8,128)S(1)} %bitcast.106, ...), kind=kLoop, calls=%fused_computation.2 | loop fusion | flops 37748736 | bytes 64690176 | tf_op jit(solution)/shard_map/mul | solution.py:192
  253.2 90.2 %fusion.4 = bf16[4,6,128,1024]{3,2,1,0:T(8,128)(2,1)} fusion(f32[4,6,2048,128]{3,2,1,0:T(8,128)} %fusion.1, f32[1024,2048,1,1]{1,0,3,2:T(8,128)S(1)} %bitcast.111), kind=kOutput, calls=%fused_computation.8 | convolution fusion | flops 38654705664 | bytes 39845888 | tf_op jit(solution)/shard_map/rp,tcpk->trck/dot_general | solution.py:205
  343.4 5.1 %fusion.27 = f32[1024,4,128]{0,2,1:T(8,128)} fusion(bf16[128,6,128,1]{0,2,1,3:T(8,128)(2,1)S(1)} %bitcast.113, bf16[4,6,128,1024]{3,2,1,0:T(8,128)(2,1)} %fusion.4), kind=kOutput, calls=%fused_computation.38 | convolution fusion | flops 805306368 | bytes 8585216 | tf_op jit(solution)/shard_map/trck,ock->rto/dot_general | solution.py:210
  348.5 1.9 copy.91
  350.4 1.6 copy.92
  352.1 7.4 %all-to-all-start.1 = ((f32[128,8,4,128]{3,1,2,0:T(8,128)}), f32[128,8,4,128]{3,1,2,0:T(8,128)S(1)}, u32[]{:S(2)}, u32[]{:S(2)}) async-start(f32[128,8,4,128]{3,1,2,0:T(8,128)} %copy.92), calls=%async_computation.1 | async-start | bytes 4194304 | tf_op jit(solution)/shard_map/all_to_all | solution.py:213
  359.5 9.0 %multiply_reduce_fusion = f32[4]{0:T(128)S(1)} fusion(f32[762,16,128]{2,1,0:T(8,128)} %param.13, f32[4]{0:T(128)S(1)} %copy-done.8, f32[762,16,128]{2,1,0:T(8,128)} %param.12), kind=kLoop, calls=%fused_computation.7 | loop fusion | flops 24969212 | bytes 12484640 | tf_op jit(solution)/shard_map/reduce_sum | solution.py:133
  368.5 21.3 %all-to-all-done.1 = f32[128,8,4,128]{3,1,2,0:T(8,128)S(1)} async-done(((f32[128,8,4,128]{3,1,2,0:T(8,128)}), f32[128,8,4,128]{3,1,2,0:T(8,128)S(1)}, u32[]{:S(2)}, u32[]{:S(2)}) %all-to-all-start.1) | async-done | bytes 2097184 | tf_op jit(solution)/shard_map/all_to_all | solution.py:213
  389.8 0.5 multiply_reduce_fusion.2
  390.4 2.7 copy.94
  393.1 0.7 collective-permute-start.7
  393.7 3.0 collective-permute-done.7
  396.7 0.7 collective-permute-start.8
  397.4 4.5 %collective-permute-done.8 = f32[2,4]{1,0:T(2,128)S(1)} collective-permute-done((f32[2,4]{1,0:T(2,128)S(1)}, f32[2,4]{1,0:T(2,128)S(1)}, u32[]{:S(2)}, u32[]{:S(2)}) %collective-permute-start.8) | collective-permute-done | bytes 64 | tf_op jit(solution)/shard_map/ppermute | solution.py:97
  402.1 3.4 collective-permute-done.9
  405.5 0.2 collective-permute-start.10
  405.7 4.8 %collective-permute-done.10 = f32[2,4]{1,0:T(2,128)S(1)} collective-permute-done((f32[2,4]{1,0:T(2,128)S(1)}, f32[2,4]{1,0:T(2,128)S(1)}, u32[]{:S(2)}, u32[]{:S(2)}) %collective-permute-start.10) | collective-permute-done | bytes 64 | tf_op jit(solution)/shard_map/ppermute | solution.py:97
  410.6 0.4 collective-permute-start.11
  411.0 3.2 collective-permute-done.11
  414.1 0.4 collective-permute-start.12
  414.6 4.7 %collective-permute-done.12 = f32[2,4]{1,0:T(2,128)S(1)} collective-permute-done((f32[2,4]{1,0:T(2,128)S(1)}, f32[2,4]{1,0:T(2,128)S(1)}, u32[]{:S(2)}, u32[]{:S(2)}) %collective-permute-start.12) | collective-permute-done | bytes 64 | tf_op jit(solution)/shard_map/ppermute | solution.py:97
  419.2 0.5 multiply_bitcast_fusion
  (76 shorter events, 2.3 us)
Async XLA Ops:
  7.2 221.2 %all-gather.2.cloned.1.call-start = ((), (), s32[]{:S(2)}) async-start(), calls=%async_computation.2 | async-start | bytes 7864320 | tf_op jit(solution)/shard_map/all_gather | solution.py:181
  14.5 6.7 %copy-start = (bf16[762,762]{1,0:T(8,128)(2,1)S(1)}, bf16[762,762]{1,0:T(8,128)(2,1)}, u32[]{:S(2)}) copy-start(bf16[762,762]{1,0:T(8,128)(2,1)} %param.15) | copy-start | bytes 3483868
  14.5 7.5 %copy-start.5 = (f32[762]{0:T(1024)S(1)}, f32[762]{0:T(1024)}, u32[]{:S(2)}) copy-start(f32[762]{0:T(1024)} %param.16) | copy-start | bytes 9148
  14.5 7.5 %copy-start.8 = (f32[4]{0:T(128)S(1)}, f32[4]{0:T(128)}, u32[]{:S(2)}) copy-start(f32[4]{0:T(128)} %param.14) | copy-start | bytes 52
  35.8 106.4 %copy-start.6 = (f32[762]{0:T(1024)S(1)}, f32[762]{0:T(1024)}, u32[]{:S(2)}) copy-start(f32[762]{0:T(1024)} %param.17) | copy-start | bytes 9148
  109.3 50.6 %copy-start.4 = (f32[1024,4]{0,1:T(4,128)S(1)}, f32[1024,4]{0,1:T(4,128)}, u32[]{:S(2)}) copy-start(f32[1024,4]{0,1:T(4,128)} %param.22) | copy-start | bytes 49156
  109.3 50.7 %copy-start.7 = (s32[1024]{0:T(1024)S(1)}, s32[1024]{0:T(1024)}, u32[]{:S(2)}) copy-start(s32[1024]{0:T(1024)} %param.21) | copy-start | bytes 12292
  109.3 58.4 %copy-start.3 = (bf16[128,762]{1,0:T(8,128)(2,1)S(1)}, bf16[128,762]{1,0:T(8,128)(2,1)}, u32[]{:S(2)}) copy-start(bf16[128,762]{1,0:T(8,128)(2,1)} %param.18) | copy-start | bytes 585220
  109.3 9.9 %collective-permute-start = (f32[4,6,16,128]{3,2,1,0:T(8,128)S(1)}, f32[4,6,16,128]{3,2,1,0:T(8,128)S(1)}, u32[]{:S(2)}, u32[]{:S(2)}) collective-permute-start(f32[4,6,16,128]{3,2,1,0:T(8,128)S(1)} %get-tuple-element.5), channel_id=1, source_target_pairs={{0,1},{1,2},{2,3},{3,4},{4,5},{5,6},{6,7},{7,8},{8,9},{9,10},{10,1... | collective-permute-start | bytes 589832 | tf_op jit(solution)/shard_map/ppermute | solution.py:89
  109.4 11.2 %collective-permute-start.1 = (f32[4,6,16,128]{3,2,1,0:T(8,128)S(1)}, f32[4,6,16,128]{3,2,1,0:T(8,128)S(1)}, u32[]{:S(2)}, u32[]{:S(2)}) collective-permute-start(f32[4,6,16,128]{3,2,1,0:T(8,128)S(1)} %get-tuple-element.5), channel_id=1, source_target_pairs={{0,2},{1,3},{2,4},{3,5},{4,6},{5,7},{6,8},{7,9},{8,10},{9,11},{10,... | collective-permute-start | bytes 589832 | tf_op jit(solution)/shard_map/ppermute | solution.py:89
  120.6 10.9 %collective-permute-start.2 = (f32[4,6,16,128]{3,2,1,0:T(8,128)S(1)}, f32[4,6,16,128]{3,2,1,0:T(8,128)S(1)}, u32[]{:S(2)}, u32[]{:S(2)}) collective-permute-start(f32[4,6,16,128]{3,2,1,0:T(8,128)S(1)} %multiply_add_fusion.3), channel_id=1, source_target_pairs={{0,2},{1,3},{2,4},{3,5},{4,6},{5,7},{6,8},{7,9},{8,10},{9,11},{10,... | collective-permute-start | bytes 589832 | tf_op jit(solution)/shard_map/ppermute | solution.py:89
  131.4 10.6 %collective-permute-start.3 = (f32[4,6,16,128]{3,2,1,0:T(8,128)S(1)}, f32[4,6,16,128]{3,2,1,0:T(8,128)S(1)}, u32[]{:S(2)}, u32[]{:S(2)}) collective-permute-start(f32[4,6,16,128]{3,2,1,0:T(8,128)S(1)} %multiply_add_fusion.2), channel_id=1, source_target_pairs={{0,4},{1,5},{2,6},{3,7},{4,8},{5,9},{6,10},{7,11},{8,12},{9,13},{1... | collective-permute-start | bytes 589832 | tf_op jit(solution)/shard_map/ppermute | solution.py:89
  142.1 7.4 %collective-permute-start.4 = (f32[4,6,16,128]{3,2,1,0:T(8,128)S(1)}, f32[4,6,16,128]{3,2,1,0:T(8,128)S(1)}, u32[]{:S(2)}, u32[]{:S(2)}) collective-permute-start(f32[4,6,16,128]{3,2,1,0:T(8,128)S(1)} %multiply_add_fusion.1), channel_id=1, source_target_pairs={{0,8},{1,9},{2,10},{3,11},{4,12},{5,13},{6,14},{7,15},{8,16},{9,17... | collective-permute-start | bytes 589832 | tf_op jit(solution)/shard_map/ppermute | solution.py:89
  149.5 7.3 %collective-permute-start.5 = (f32[4,6,16,128]{3,2,1,0:T(8,128)S(1)}, f32[4,6,16,128]{3,2,1,0:T(8,128)S(1)}, u32[]{:S(2)}, u32[]{:S(2)}) collective-permute-start(f32[4,6,16,128]{3,2,1,0:T(8,128)S(1)} %multiply_add_fusion), channel_id=1, source_target_pairs={{0,16},{1,17},{2,18},{3,19},{4,20},{5,21},{6,22},{7,23},{8,24},{9,... | collective-permute-start | bytes 589832 | tf_op jit(solution)/shard_map/ppermute | solution.py:89
  161.2 19.8 %all-to-all-start = ((f32[128,8,5]{1,2,0:T(8,128)}), f32[128,8,5]{1,2,0:T(8,128)S(1)}, u32[]{:S(2)}, u32[]{:S(2)}) async-start(f32[128,8,5]{1,2,0:T(8,128)} %copy.86), calls=%async_computation | async-start | bytes 1048576 | tf_op jit(solution)/shard_map/all_to_all | solution.py:130
  232.9 20.3 %slice-start = ((s8[8388608]{0:T(1024)(128)(4,1)}), s8[4194304]{0:T(1024)(128)(4,1)S(1)}, s32[]{:S(2)}) async-start(s8[8388608]{0:T(1024)(128)(4,1)} %bitcast.110), calls=%async_computation.3 | async-start | bytes 8388608
  233.3 19.9 %slice-start.1 = ((s8[8388608]{0:T(1024)(128)(4,1)}), s8[4194304]{0:T(1024)(128)(4,1)S(1)}, s32[]{:S(2)}) async-start(s8[8388608]{0:T(1024)(128)(4,1)} %bitcast.110), calls=%async_computation.4 | async-start | bytes 8388608
  348.5 10.9 %copy-start.9 = (s32[1,128]{1,0:T(1,128)S(1)}, s32[1,128]{1,0:T(1,128)}, u32[]{:S(2)}) copy-start(s32[1,128]{1,0:T(1,128)} %param.23) | copy-start | bytes 1540
  352.0 37.7 %copy-start.1 = (f32[1024,128]{1,0:T(8,128)S(1)}, f32[1024,128]{1,0:T(8,128)}, u32[]{:S(2)}) copy-start(f32[1024,128]{1,0:T(8,128)} %param.20) | copy-start | bytes 1572868
  352.0 37.7 %copy-start.2 = (f32[1024,128]{1,0:T(8,128)S(1)}, f32[1024,128]{1,0:T(8,128)}, u32[]{:S(2)}) copy-start(f32[1024,128]{1,0:T(8,128)} %param.19) | copy-start | bytes 1572868
  352.1 37.7 %all-to-all-start.1 = ((f32[128,8,4,128]{3,1,2,0:T(8,128)}), f32[128,8,4,128]{3,1,2,0:T(8,128)S(1)}, u32[]{:S(2)}, u32[]{:S(2)}) async-start(f32[128,8,4,128]{3,1,2,0:T(8,128)} %copy.92), calls=%async_computation.1 | async-start | bytes 4194304 | tf_op jit(solution)/shard_map/all_to_all | solution.py:213
  390.3 2.8 collective-permute-start.6
  393.1 3.7 collective-permute-start.7
  396.7 5.2 %collective-permute-start.8 = (f32[2,4]{1,0:T(2,128)S(1)}, f32[2,4]{1,0:T(2,128)S(1)}, u32[]{:S(2)}, u32[]{:S(2)}) collective-permute-start(f32[2,4]{1,0:T(2,128)S(1)} %fusion.41), channel_id=1, source_target_pairs={{0,4},{1,5},{2,6},{3,7},{4,0},{5,1},{6,2},{7,3},{8,12},{9,13},{10,... | collective-permute-start | bytes 104 | tf_op jit(solution)/shard_map/ppermute | solution.py:97
  401.9 3.6 collective-permute-start.9
  405.5 5.1 %collective-permute-start.10 = (f32[2,4]{1,0:T(2,128)S(1)}, f32[2,4]{1,0:T(2,128)S(1)}, u32[]{:S(2)}, u32[]{:S(2)}) collective-permute-start(f32[2,4]{1,0:T(2,128)S(1)} %add.375), channel_id=1, source_target_pairs={{0,16},{1,17},{2,18},{3,19},{4,20},{5,21},{6,22},{7,23},{8,24},{9,... | collective-permute-start | bytes 104 | tf_op jit(solution)/shard_map/ppermute | solution.py:97
  410.6 3.6 collective-permute-start.11
  414.1 5.1 %collective-permute-start.12 = (f32[2,4]{1,0:T(2,128)S(1)}, f32[2,4]{1,0:T(2,128)S(1)}, u32[]{:S(2)}, u32[]{:S(2)}) collective-permute-start(f32[2,4]{1,0:T(2,128)S(1)} %add.377), channel_id=1, source_target_pairs={{0,64},{32,96},{64,0},{96,32},{1,65},{33,97},{65,1},{97,33},{2,66}... | collective-permute-start | bytes 104 | tf_op jit(solution)/shard_map/ppermute | solution.py:97
Sparse Core Ops, SparseCore 0:
  160.0 68.3 all-gather.1
